TPU v7x, 128 devices: a whole 4x4x4 slice. The times are simulated.
128 devices in a mesh: ctx: 32 (over z, y, core), head: 4 (over x).
Axes of the slice: x: 4, y: 4, z: 4, core: 2. Of those that a mesh axis runs over, the one named last changes fastest.
Arguments:
- tokens: bfloat16 [12288, 3840], P(('ctx', 'head'))
- w_query: bfloat16 [3840, 4096], P(None, 'head')
- w_key: bfloat16 [3840, 2048], P(None, 'head')
- w_value: bfloat16 [3840, 2048], P(None, 'head'), may hold values from -0.09375 to 0.09375
- query_gain: float32 [256], replicated
- key_gain: float32 [256], replicated
- positions: int32 [12288], P('ctx'), may hold values from 0 to 3071, as said below
- out_grad: bfloat16 [12288, 4096], P('ctx', 'head'), may hold values from -6 to 6
Outputs:
- attended: bfloat16 [12288, 4096], P('ctx', 'head')
- input_grad: bfloat16 [12288, 3840], P(('ctx', 'head'))
- grad_query: bfloat16 [3840, 4096], P('ctx', 'head')
- grad_key: bfloat16 [3840, 2048], P('ctx', 'head')
- grad_value: bfloat16 [3840, 2048], P('ctx', 'head')
Inputs may be any that keep to these rules, and one draw needn't show every extreme that they name: `positions`: positions rise by one from token to token inside a document and are 0 at a document's first token; the window's first document began before the window; no document that starts inside the window is longer than 2048 tokens.
All inputs are finite; a program needn't handle non-finite values.
Results may differ from a plain program's by a relative error of at most 0.04.
The roundings to bfloat16 on the way count: a program that leaves them out, or rounds other values in their place, can miss the bound.
Values may be sent and summed in bfloat16 or wider, within the bound.
No kernel may reach another device: no remote copies, remote signals or barrier semaphores. Data moves between devices by JAX's collectives and lax.ppermute only.
A program may use at most 192 MiB of HBM per device.

v0:
```python
from functools import reduce
import math

import jax
import jax.numpy as jnp
from jax import lax
from jax.experimental import pallas as pl
from jax.experimental.pallas import tpu as pltpu
from jax.sharding import PartitionSpec as P

WINDOW = 1024


norm_eps = 1e-06
rope_base = 10000.0


def passed_along(block, axis, distance):
    devices = range(lax.axis_size(axis))
    route = [(i - distance, i) for i in devices if i - distance in devices]
    return lax.ppermute(block, axis, route)


CORES = 2
Y_CHIPS = 4


def ring_pairs(rank_count, along_y):
    z_chips = rank_count // (CORES * Y_CHIPS)
    forward = []
    for z in range(z_chips):
        for y in range(Y_CHIPS):
            for core in range(CORES):
                source = (z * Y_CHIPS + y) * CORES + core
                if along_y:
                    target = (z * Y_CHIPS + (y + 1) % Y_CHIPS) * CORES + core
                else:
                    target = (((z + 1) % z_chips) * Y_CHIPS + y) * CORES + core
                forward.append((source, target))
    backward = [(target, source) for source, target in forward]
    return forward, backward


def ring_reduce_scatter(parts, axis, position, forward, backward):
    count = parts.shape[axis]
    half = parts.shape[-1] // 2

    def own(index, low):
        piece = lax.slice_in_dim(parts, low, low + half, axis=parts.ndim - 1)
        return lax.dynamic_index_in_dim(piece, index % count, axis, keepdims=False)

    up = own(position + count - 1, 0)
    down = own(position + 1, half)
    for step in range(count - 1):
        up = lax.ppermute(up.astype(jnp.bfloat16), "ctx", forward).astype(jnp.float32) + own(
            position + 2 * count - step - 2, 0
        )
        down = lax.ppermute(down.astype(jnp.bfloat16), "ctx", backward).astype(
            jnp.float32
        ) + own(position + step + 2, half)
    return jnp.concatenate([up, down], axis=-1)


def pair_rows(gathered, core, rank_count):
    z_chips = rank_count // (CORES * Y_CHIPS)
    count, width = gathered.shape
    grid = gathered.reshape(count, z_chips, Y_CHIPS, CORES, width // rank_count)
    return lax.dynamic_index_in_dim(grid, core, 3, keepdims=False).reshape(count, width // CORES)


def rounded_term(rows, columns):
    return (
        lax.dot_general(rows, columns, (((0,), (0,)), ((), ())), preferred_element_type=jnp.float32)
        .astype(jnp.bfloat16)
        .astype(jnp.float32)
    )


def torus_reduce_scatter(pair_sum, my_rank, rank_count):
    z_chips = rank_count // (CORES * Y_CHIPS)
    rows, columns = pair_sum.shape
    y_pos = (my_rank // CORES) % Y_CHIPS
    z_pos = my_rank // (CORES * Y_CHIPS)
    grid = pair_sum.reshape(z_chips, Y_CHIPS, rows // (z_chips * Y_CHIPS), columns)
    y_forward, y_backward = ring_pairs(rank_count, True)
    z_forward, z_backward = ring_pairs(rank_count, False)
    half = columns // 2
    first = grid[..., :half]
    second = grid[..., half:]
    first = ring_reduce_scatter(first, 1, y_pos, y_forward, y_backward)
    first = ring_reduce_scatter(first, 0, z_pos, z_forward, z_backward)
    second = ring_reduce_scatter(second, 0, z_pos, z_forward, z_backward)
    second = ring_reduce_scatter(second, 0, y_pos, y_forward, y_backward)
    return jnp.concatenate([first, second], axis=-1)


def attention_body(q_ref, k_ref, v_ref, do_ref, lo_ref, att_ref, dq_ref, dk_ref, dv_ref):
    rows = q_ref.shape[0]
    keys, width = k_ref.shape
    k = k_ref[...]
    v = v_ref[...]
    key_index = lax.broadcasted_iota(jnp.int32, (rows, keys), 1)
    query_index = lax.broadcasted_iota(jnp.int32, (rows, keys), 0)
    visible = (key_index >= lo_ref[...]) & (key_index <= query_index + (keys - rows))
    dk = jnp.zeros((keys, width), jnp.float32)
    dv = jnp.zeros((keys, width), jnp.float32)
    for head in range(q_ref.shape[1] // width):
        cols = slice(head * width, (head + 1) * width)
        q = q_ref[:, cols]
        do = do_ref[:, cols]
        scores = lax.dot_general(q, k, (((1,), (1,)), ((), ())), preferred_element_type=jnp.float32)
        peak = jnp.max(jnp.where(visible, scores, -jnp.inf), axis=-1, keepdims=True)
        weights = jnp.where(visible, jnp.exp(scores - peak), 0.0)
        probs = weights / jnp.sum(weights, axis=-1, keepdims=True)
        probs_bf16 = probs.astype(jnp.bfloat16)
        attended = jnp.dot(probs_bf16, v, preferred_element_type=jnp.float32).astype(jnp.bfloat16)
        att_ref[:, cols] = attended
        delta = jnp.sum(
            do.astype(jnp.float32) * attended.astype(jnp.float32), axis=-1, keepdims=True
        )
        dprobs = lax.dot_general(do, v, (((1,), (1,)), ((), ())), preferred_element_type=jnp.float32)
        dscores = (probs * (dprobs - delta)).astype(jnp.bfloat16)
        dq_ref[:, cols] = jnp.dot(dscores, k, preferred_element_type=jnp.float32)
        dk = dk + lax.dot_general(
            dscores, q, (((0,), (0,)), ((), ())), preferred_element_type=jnp.float32
        )
        dv = dv + lax.dot_general(
            probs_bf16, do, (((0,), (0,)), ((), ())), preferred_element_type=jnp.float32
        )
    dk_ref[...] = dk
    dv_ref[...] = dv


def fused_attention(q2d, k_all, v_all, do2d, lower, groups):
    rows, query_cols = q2d.shape
    keys, kv_cols = k_all.shape
    width = kv_cols // groups
    per_group = query_cols // groups
    heads = query_cols // width
    flops = 2 * rows * keys * width * 6 * heads
    io_bytes = 2 * (3 * rows * query_cols + 2 * keys * kv_cols) + 4 * (rows * query_cols + 2 * keys * kv_cols)
    return pl.pallas_call(
        attention_body,
        grid=(groups,),
        in_specs=[
            pl.BlockSpec((rows, per_group), lambda g: (0, g)),
            pl.BlockSpec((keys, width), lambda g: (0, g)),
            pl.BlockSpec((keys, width), lambda g: (0, g)),
            pl.BlockSpec((rows, per_group), lambda g: (0, g)),
            pl.BlockSpec((rows, 1), lambda g: (0, 0)),
        ],
        out_specs=[
            pl.BlockSpec((rows, per_group), lambda g: (0, g)),
            pl.BlockSpec((rows, per_group), lambda g: (0, g)),
            pl.BlockSpec((keys, width), lambda g: (0, g)),
            pl.BlockSpec((keys, width), lambda g: (0, g)),
        ],
        out_shape=[
            jax.ShapeDtypeStruct((rows, query_cols), jnp.bfloat16),
            jax.ShapeDtypeStruct((rows, query_cols), jnp.float32),
            jax.ShapeDtypeStruct((keys, kv_cols), jnp.float32),
            jax.ShapeDtypeStruct((keys, kv_cols), jnp.float32),
        ],
        compiler_params=pltpu.CompilerParams(vmem_limit_bytes=56 * 1024 * 1024),
        cost_estimate=pl.CostEstimate(
            flops=flops, transcendentals=rows * keys * heads, bytes_accessed=io_bytes
        ),
    )(q2d, k_all, v_all, do2d, lower)


def rope_tables(positions, head_width):
    half_width = head_width // 2
    indices = jnp.arange(half_width, dtype=jnp.float32)
    frequency = jnp.power(rope_base, -2.0 * indices / head_width)
    angles = positions.astype(jnp.float32)[:, None] * frequency[None, :]
    return (jnp.cos(angles)[:, None, :], jnp.sin(angles)[:, None, :])


def rotate(vector, cosine_table, sine_table):
    half_width = vector.shape[-1] // 2
    lower_half = vector[..., :half_width]
    upper_half = vector[..., half_width:]
    return jnp.concatenate(
        [
            lower_half * cosine_table - upper_half * sine_table,
            upper_half * cosine_table + lower_half * sine_table,
        ],
        axis=-1,
    )


def unrotate(rotated, cosine_table, sine_table):
    half_width = rotated.shape[-1] // 2
    lower_half = rotated[..., :half_width]
    upper_half = rotated[..., half_width:]
    return jnp.concatenate(
        [
            lower_half * cosine_table + upper_half * sine_table,
            upper_half * cosine_table - lower_half * sine_table,
        ],
        axis=-1,
    )


def normalize(vector, gain_vector):
    inv_rms = lax.rsqrt(jnp.mean(vector * vector, axis=-1, keepdims=True) + norm_eps)
    return (vector * inv_rms * gain_vector, inv_rms)


def norm_back(vector, inv_rms, gain_vector, upstream):
    scaled = upstream * gain_vector
    return inv_rms * scaled - vector * (inv_rms * inv_rms * inv_rms) * jnp.mean(
        vector * scaled, axis=-1, keepdims=True
    )


def on_device(tokens, w_query, w_key, w_value, query_gain, key_gain, positions, out_grad):
    gathered = lax.all_gather(tokens, "head", axis=0, tiled=True)
    row_count = gathered.shape[0]
    head_width = query_gain.shape[0]
    head_count = w_query.shape[1] // head_width
    groups = w_key.shape[1] // head_width
    group_size = head_count // groups
    rank_count = lax.axis_size("ctx")
    my_rank = lax.axis_index("ctx")
    reach_blocks = min((WINDOW - 2) // row_count + 1, rank_count - 1)
    core = my_rank % CORES
    partner = [(rank, rank ^ 1) for rank in range(rank_count)]
    my_rows = pair_rows(gathered, core, rank_count)
    partner_rows = lax.ppermute(
        pair_rows(gathered, CORES - 1 - core, rank_count), "ctx", partner
    )
    query_scale = 1.0 / math.sqrt(head_width)
    query_raw = jnp.dot(gathered, w_query, preferred_element_type=jnp.float32).reshape(
        row_count, head_count, head_width
    )
    key_raw = jnp.dot(gathered, w_key, preferred_element_type=jnp.float32).reshape(
        row_count, groups, head_width
    )
    value_states = jnp.dot(gathered, w_value, preferred_element_type=jnp.float32).astype(
        jnp.bfloat16
    )
    cosine_table, sine_table = rope_tables(positions, head_width)
    query_normed, query_inv = normalize(query_raw, query_gain)
    key_normed, key_inv = normalize(key_raw, key_gain)
    query_states = (
        (rotate(query_normed, cosine_table, sine_table) * query_scale)
        .astype(jnp.bfloat16)
        .reshape(row_count, groups, group_size, head_width)
    )
    key_states = (
        rotate(key_normed, cosine_table, sine_table)
        .astype(jnp.bfloat16)
        .reshape(row_count, groups * head_width)
    )
    local_kv = jnp.stack([key_states, value_states])
    blocks = [local_kv] + [
        passed_along(local_kv, "ctx", stride) for stride in range(1, reach_blocks + 1)
    ]
    offsets = jnp.arange(row_count, dtype=jnp.int32)
    key_count = (reach_blocks + 1) * row_count
    lower = jnp.maximum(
        (reach_blocks - my_rank) * row_count,
        reach_blocks * row_count + offsets - jnp.minimum(positions, WINDOW - 1),
    )[:, None]
    ordered = blocks[::-1]
    all_keys = jnp.concatenate([block[0] for block in ordered], axis=0)
    all_values = jnp.concatenate([block[1] for block in ordered], axis=0)
    attended, query_grads, key_grad_all, value_grad_all = fused_attention(
        query_states.reshape(row_count, head_count * head_width),
        all_keys,
        all_values,
        out_grad,
        lower,
        groups,
    )

    def grad_rows(stride):
        start = key_count - (stride + 1) * row_count
        return jnp.stack(
            [
                key_grad_all[start : start + row_count],
                value_grad_all[start : start + row_count],
            ]
        )

    key_grad_parts = [grad_rows(stride) for stride in range(reach_blocks + 1)]
    returned = reduce(
        jnp.add,
        [key_grad_parts[0]]
        + [
            passed_along(key_grad_parts[stride].astype(jnp.bfloat16), "ctx", -stride).astype(
                jnp.float32
            )
            for stride in range(1, reach_blocks + 1)
        ],
    )
    key_grads = returned[0].reshape(row_count, groups, head_width)
    value_grads = returned[1].astype(jnp.bfloat16)
    query_raw_grad = (
        norm_back(
            query_raw,
            query_inv,
            query_gain,
            unrotate(
                query_grads.reshape(row_count, head_count, head_width), cosine_table, sine_table
            )
            * query_scale,
        )
        .astype(jnp.bfloat16)
        .reshape(row_count, head_count * head_width)
    )
    key_raw_grad = (
        norm_back(key_raw, key_inv, key_gain, unrotate(key_grads, cosine_table, sine_table))
        .astype(jnp.bfloat16)
        .reshape(row_count, groups * head_width)
    )
    input_terms = (
        jnp.dot(query_raw_grad, w_query.T, preferred_element_type=jnp.float32)
        + jnp.dot(key_raw_grad, w_key.T, preferred_element_type=jnp.float32)
        + jnp.dot(value_grads, w_value.T, preferred_element_type=jnp.float32)
    )
    input_grad = lax.psum_scatter(
        input_terms.astype(jnp.bfloat16), "head", scatter_dimension=0, tiled=True
    )
    grad_columns = jnp.concatenate([query_raw_grad, key_raw_grad, value_grads], axis=1)
    partner_columns = lax.ppermute(grad_columns, "ctx", partner)
    pair_sum = rounded_term(my_rows, grad_columns) + rounded_term(partner_rows, partner_columns)
    summed = torus_reduce_scatter(pair_sum, my_rank, rank_count).astype(jnp.bfloat16)
    query_cols = head_count * head_width
    key_cols = groups * head_width
    return (
        attended.reshape(row_count, query_cols),
        input_grad,
        summed[:, :query_cols],
        summed[:, query_cols : query_cols + key_cols],
        summed[:, query_cols + key_cols :],
    )


def solution(mesh):
    in_specs = (
        P(("ctx", "head"), None),
        P(None, "head"),
        P(None, "head"),
        P(None, "head"),
        P(),
        P(),
        P("ctx"),
        P("ctx", "head"),
    )
    out_specs = (
        P("ctx", "head"),
        P(("ctx", "head"), None),
        P("ctx", "head"),
        P("ctx", "head"),
        P("ctx", "head"),
    )
    return jax.shard_map(
        on_device, mesh=mesh, in_specs=in_specs, out_specs=out_specs, check_vma=False
    )
```

profile of v0, /device:TPU:0, one launch (start us, length us, event | category | flops | bytes accessed | tf_op | source)
XLA Modules:
  0.0 316.8 jit_solution(16124017693748697715)
XLA Ops:
  13.1 36.9 %all-gather.2.cloned.1.call-done = bf16[384,3840]{1,0:T(8,128)(2,1)} async-done(((bf16[96,3840]{1,0:T(8,128)(2,1)}), bf16[384,3840]{1,0:T(8,128)(2,1)}) %all-gather.2.cloned.1.call-update) | async-done | bytes 2949136 | tf_op jit(solution)/shard_map/all_gather | solution.py:218
  50.0 4.7 %fusion.37 = f32[384,512]{1,0:T(8,128)S(1)} fusion(bf16[384,3840]{1,0:T(8,128)(2,1)} %all-gather.2.cloned.1.call-done, bf16[3840,512]{1,0:T(8,128)(2,1)} %param.10), kind=kOutput, calls=%fused_computation.131 | convolution fusion | flops 1509949440 | bytes 7667712 | tf_op jit(solution)/shard_map/dot_general | solution.py:237
  58.2 4.8 %convolution_convert_fusion = bf16[384,512]{1,0:T(8,128)(2,1)S(1)} fusion(bf16[384,3840]{1,0:T(8,128)(2,1)} %all-gather.2.cloned.1.call-done, bf16[3840,512]{1,0:T(8,128)(2,1)} %param.11), kind=kOutput, calls=%fused_computation.17 | convolution fusion | flops 1510146048 | bytes 7274496 | tf_op jit(solution)/shard_map/dot_general | solution.py:240
  64.7 2.5 collective-permute-start.2
  67.2 3.8 %collective-permute-start.1 = (bf16[2,384,512]{2,1,0:T(8,128)(2,1)}, bf16[2,384,512]{2,1,0:T(8,128)(2,1)}, u32[]{:S(2)}, u32[]{:S(2)}) collective-permute-start(bf16[2,384,512]{2,1,0:T(8,128)(2,1)} %pad_maximum_fusion.4), channel_id=1, source_target_pairs={{0,8},{4,12},{8,16},{12,20},{16,24},{20,28},{24,32},{28,36},{32,40... | collective-permute-start | bytes 2359304 | tf_op jit(solution)/shard_map/ppermute | solution.py:21
  71.0 4.4 %collective-permute-start = (bf16[2,384,512]{2,1,0:T(8,128)(2,1)}, bf16[2,384,512]{2,1,0:T(8,128)(2,1)}, u32[]{:S(2)}, u32[]{:S(2)}) collective-permute-start(bf16[2,384,512]{2,1,0:T(8,128)(2,1)} %pad_maximum_fusion.4), channel_id=1, source_target_pairs={{0,12},{4,16},{8,20},{12,24},{16,28},{20,32},{24,36},{28,40},{32,4... | collective-permute-start | bytes 2359304 | tf_op jit(solution)/shard_map/ppermute | solution.py:21
  75.3 7.7 %fusion.36 = f32[384,1024]{1,0:T(8,128)} fusion(bf16[384,3840]{1,0:T(8,128)(2,1)S(1)} %copy-done.13, bf16[3840,1024]{1,0:T(8,128)(2,1)} %param.9), kind=kOutput, calls=%fused_computation.130 | convolution fusion | flops 3019898880 | bytes 12386304 | tf_op jit(solution)/shard_map/dot_general | solution.py:234
  83.1 2.0 reshape.160
  91.6 1.5 copy.52
  93.6 1.5 copy.49
  98.0 4.5 %copy.40 = bf16[384,3840]{0,1:T(8,128)(2,1)} copy(bf16[384,3840]{1,0:T(8,128)(2,1)} %all-gather.2.cloned.1.call-done) | data formatting | bytes 5898240 | tf_op jit(solution)/shard_map/all_gather | solution.py:218
  102.6 3.8 %constant_dynamic-slice_fusion = (bf16[384,4,4,1,120]{0,4,3,2,1:T(8,128)(2,1)}, bf16[384,4,4,1,120]{0,4,3,2,1:T(8,128)(2,1)}) fusion(bf16[384,4,4,2,120]{0,4,3,2,1:T(8,128)(2,1)} %bitcast.191, s32[]{:T(128)S(6)} %select_n.174, s32[]{:T(128)S(6)} %select_n.173), kind=kLoop, calls=%fused_computation.118 | loop fusion | bytes 5898248 | tf_op jit(solution)/shard_map/jit(dynamic_index_in_dim)/dynamic_slice | solution.py:68
  111.1 1.8 pad_maximum_fusion
  112.9 14.7 %shard_map.119 = (bf16[384,1024]{1,0:T(8,128)(2,1)}, f32[384,1024]{1,0:T(8,128)}, f32[1536,512]{1,0:T(8,128)}, f32[1536,512]{1,0:T(8,128)}) custom-call(bf16[384,1024]{1,0:T(8,128)(2,1)} %bitcast.213, bf16[1536,512]{1,0:T(8,128)(2,1)} %get-tuple-element.51.k_ref, bf16[1536,512]{1,0:T(8,128)(2,1)} %get-tuple-element.52.v_ref, bf16[384,1024]{1,0:T(8,128)(2,1)} %do_ref.1, ...), custom_call_target="tpu_custom_call" | custom-call | flops 7247757312 | bytes 13369344 | tf_op jit(solution)/shard_map/pallas_call | solution.py:142
  128.8 3.2 %convert.34 = bf16[1536,512]{1,0:T(8,128)(2,1)} convert(f32[1536,512]{1,0:T(8,128)} %get-tuple-element.12) | non-fusion elementwise | flops 786432 | bytes 4718592 | tf_op jit(solution)/shard_map/convert.20
  132.1 2.9 reshape.162
  135.0 1.9 multiply_add_fusion
  141.4 1.5 collective-permute-start.3
  146.8 1.8 subtract_convert_fusion
  148.6 9.8 %collective-permute-done.5 = bf16[2,384,512]{2,1,0:T(8,128)(2,1)S(1)} collective-permute-done((bf16[2,384,512]{2,1,0:T(8,128)(2,1)S(1)}, bf16[2,384,512]{2,1,0:T(8,128)(2,1)S(1)}, u32[]{:S(2)}, u32[]{:S(2)}) %collective-permute-start.5) | collective-permute-done | bytes 786464 | tf_op jit(solution)/shard_map/ppermute | solution.py:21
  158.4 3.9 %collective-permute-done.4 = bf16[2,384,512]{2,1,0:T(8,128)(2,1)S(1)} collective-permute-done((bf16[2,384,512]{2,1,0:T(8,128)(2,1)S(1)}, bf16[2,384,512]{2,1,0:T(8,128)(2,1)S(1)}, u32[]{:S(2)}, u32[]{:S(2)}) %collective-permute-start.4) | collective-permute-done | bytes 786464 | tf_op jit(solution)/shard_map/ppermute | solution.py:21
  164.9 1.5 multiply_add_fusion.2
  169.2 15.0 %collective-permute-start.7 = (bf16[384,2048]{1,0:T(8,128)(2,1)S(1)}, bf16[384,2048]{1,0:T(8,128)(2,1)S(1)}, u32[]{:S(2)}, u32[]{:S(2)}) collective-permute-start(bf16[384,2048]{1,0:T(8,128)(2,1)S(1)} %pad_maximum_fusion.3), channel_id=1, source_target_pairs={{0,4},{4,0},{8,12},{12,8},{16,20},{20,16},{24,28},{28,24},{32,36},... | collective-permute-start | bytes 4718600 | tf_op jit(solution)/shard_map/ppermute | solution.py:327
  184.3 5.8 %fusion.38 = f32[384,3840]{1,0:T(8,128)S(1)} fusion(bf16[384,1024]{1,0:T(8,128)(2,1)S(1)} %copy-done.12, bf16[3840,1024]{1,0:T(8,128)(2,1)} %param.9), kind=kOutput, calls=%fused_computation.132 | convolution fusion | flops 3019898880 | bytes 14548992 | tf_op jit(solution)/shard_map/dot_general | solution.py:319
  190.1 6.2 %fusion.33 = bf16[1920,2048]{1,0:T(8,128)(2,1)S(1)} fusion(bf16[384,1920]{0,1:T(8,128)(2,1)} %bitcast.212, bf16[384,512]{1,0:T(8,128)(2,1)S(1)} %copy-done.17, bf16[384,512]{1,0:T(8,128)(2,1)S(1)} %subtract_convert_fusion.1, bf16[384,1024]{1,0:T(8,128)(2,1)S(1)} %copy-done.12), kind=kOutput, calls=%fused_computation.128 | convolution fusion | flops 3024617472 | bytes 10911744 | tf_op jit(solution)/shard_map/dot_general | solution.py:73
  196.3 4.2 %convolution_add_fusion.1 = f32[384,3840]{1,0:T(8,128)} fusion(f32[384,3840]{1,0:T(8,128)S(1)} %fusion.38, bf16[384,512]{1,0:T(8,128)(2,1)S(1)} %subtract_convert_fusion.1, bf16[3840,512]{1,0:T(8,128)(2,1)S(1)} %copy-done.7), kind=kOutput, calls=%fused_computation.2 | convolution fusion | flops 1511424000 | bytes 16121856 | tf_op jit(solution)/shard_map/dot_general | solution.py:320
  200.6 9.0 %convert_add_fusion = f32[1920,2048]{1,0:T(8,128)} fusion(bf16[1920,2048]{1,0:T(8,128)(2,1)S(1)} %fusion.33, bf16[384,1920]{0,1:T(8,128)(2,1)} %collective-permute-done.6, bf16[384,2048]{1,0:T(8,128)(2,1)S(1)} %collective-permute-done.7), kind=kOutput, calls=%fused_computation | convolution fusion | flops 3035627520 | bytes 26640384 | tf_op jit(solution)/shard_map/dot_general | solution.py:73
  209.6 12.6 %fusion.34 = (f32[4,4,120,512]{3,2,1,0:T(8,128)}, f32[4,4,120,512]{3,2,1,0:T(8,128)}, f32[4,4,120,512]{3,2,1,0:T(8,128)}, f32[4,4,120,512]{3,2,1,0:T(8,128)}) fusion(f32[4,4,120,2048]{3,2,1,0:T(8,128)} %bitcast.190), kind=kLoop, calls=%fused_computation.129 | loop fusion | bytes 31457280 | tf_op jit(solution)/shard_map/slice | solution.py:49
  223.4 12.1 %collective-permute-start.14 = (bf16[4,120,512]{2,1,0:T(8,128)(2,1)S(1)}, bf16[4,120,512]{2,1,0:T(8,128)(2,1)S(1)}, u32[]{:S(2)}, u32[]{:S(2)}) collective-permute-start(bf16[4,120,512]{2,1,0:T(8,128)(2,1)S(1)} %fusion.12), channel_id=1, source_target_pairs={{8,0},{12,4},{16,8},{20,12},{24,16},{28,20},{0,24},{4,28},{40,32},... | collective-permute-start | bytes 1474568 | tf_op jit(solution)/shard_map/ppermute | solution.py:58
  235.5 7.2 %fusion = bf16[384,3840]{1,0:T(8,128)(2,1)} fusion(f32[384,3840]{1,0:T(8,128)} %convolution_add_fusion.1, bf16[3840,512]{1,0:T(8,128)(2,1)} %param.11, f32[2,384,512]{2,1,0:T(8,128)S(1)} %fusion.3), kind=kOutput, calls=%fused_computation.3 | convolution fusion | flops 1512898560 | bytes 13172736 | tf_op jit(solution)/shard_map/dot_general | solution.py:321
  245.5 1.6 collective-permute-start.20
  248.4 2.0 collective-permute-start.26
  251.8 3.3 %collective-permute-start.15 = (bf16[4,120,512]{2,1,0:T(8,128)(2,1)S(1)}, bf16[4,120,512]{2,1,0:T(8,128)(2,1)S(1)}, u32[]{:S(2)}, u32[]{:S(2)}) collective-permute-start(bf16[4,120,512]{2,1,0:T(8,128)(2,1)S(1)} %fusion.11), channel_id=1, source_target_pairs={{8,0},{12,4},{16,8},{20,12},{24,16},{28,20},{0,24},{4,28},{40,32},... | collective-permute-start | bytes 1474568 | tf_op jit(solution)/shard_map/ppermute | solution.py:58
  255.0 3.1 collective-permute-done.8
  259.8 1.6 collective-permute-start.21
  261.6 2.9 collective-permute-start.27
  266.0 3.7 %collective-permute-start.16 = (bf16[4,120,512]{2,1,0:T(8,128)(2,1)S(1)}, bf16[4,120,512]{2,1,0:T(8,128)(2,1)S(1)}, u32[]{:S(2)}, u32[]{:S(2)}) collective-permute-start(bf16[4,120,512]{2,1,0:T(8,128)(2,1)S(1)} %fusion.10), channel_id=1, source_target_pairs={{8,0},{12,4},{16,8},{20,12},{24,16},{28,20},{0,24},{4,28},{40,32},... | collective-permute-start | bytes 1474568 | tf_op jit(solution)/shard_map/ppermute | solution.py:58
  269.7 3.2 %collective-permute-done.9 = bf16[4,120,512]{2,1,0:T(8,128)(2,1)S(1)} collective-permute-done((bf16[4,120,512]{2,1,0:T(8,128)(2,1)S(1)}, bf16[4,120,512]{2,1,0:T(8,128)(2,1)S(1)}, u32[]{:S(2)}, u32[]{:S(2)}) %collective-permute-start.9) | collective-permute-done | bytes 491552 | tf_op jit(solution)/shard_map/ppermute | solution.py:55
  273.4 1.6 collective-permute-start.22
  275.1 2.6 collective-permute-start.28
  280.6 5.1 %collective-permute-done.10 = bf16[4,120,512]{2,1,0:T(8,128)(2,1)S(1)} collective-permute-done((bf16[4,120,512]{2,1,0:T(8,128)(2,1)S(1)}, bf16[4,120,512]{2,1,0:T(8,128)(2,1)S(1)}, u32[]{:S(2)}, u32[]{:S(2)}) %collective-permute-start.10) | collective-permute-done | bytes 491552 | tf_op jit(solution)/shard_map/ppermute | solution.py:55
  285.9 1.6 collective-permute-start.11
  288.0 3.3 %collective-permute-start.29 = (bf16[120,512]{1,0:T(8,128)(2,1)S(1)}, bf16[120,512]{1,0:T(8,128)(2,1)S(1)}, u32[]{:S(2)}, u32[]{:S(2)}) collective-permute-start(bf16[120,512]{1,0:T(8,128)(2,1)S(1)} %fusion.32), channel_id=1, source_target_pairs={{8,0},{12,4},{16,8},{20,12},{24,16},{28,20},{0,24},{4,28},{40,32},... | collective-permute-start | bytes 368648 | tf_op jit(solution)/shard_map/ppermute | solution.py:58
  291.3 2.7 collective-permute-start.18
  294.4 3.5 %collective-permute-start.30 = (bf16[120,512]{1,0:T(8,128)(2,1)S(1)}, bf16[120,512]{1,0:T(8,128)(2,1)S(1)}, u32[]{:S(2)}, u32[]{:S(2)}) collective-permute-start(bf16[120,512]{1,0:T(8,128)(2,1)S(1)} %fusion.19), channel_id=1, source_target_pairs={{8,0},{12,4},{16,8},{20,12},{24,16},{28,20},{0,24},{4,28},{40,32},... | collective-permute-start | bytes 368648 | tf_op jit(solution)/shard_map/ppermute | solution.py:58
  297.9 3.0 collective-permute-start.19
  301.6 3.6 %collective-permute-start.31 = (bf16[120,512]{1,0:T(8,128)(2,1)S(1)}, bf16[120,512]{1,0:T(8,128)(2,1)S(1)}, u32[]{:S(2)}, u32[]{:S(2)}) collective-permute-start(bf16[120,512]{1,0:T(8,128)(2,1)S(1)} %fusion.18), channel_id=1, source_target_pairs={{8,0},{12,4},{16,8},{20,12},{24,16},{28,20},{0,24},{4,28},{40,32},... | collective-permute-start | bytes 368648 | tf_op jit(solution)/shard_map/ppermute | solution.py:58
  305.2 2.2 collective-permute-done.13
  (189 shorter events, 57.5 us)
Async XLA Ops:
  7.2 42.8 %all-gather.2.cloned.1.call-start = ((), (), s32[]{:S(2)}) async-start(), calls=%async_computation.1 | async-start | bytes 3686400 | tf_op jit(solution)/shard_map/all_gather | solution.py:218
  7.9 301.8 %reduce-scatter.2.cloned.1.call-start = ((), (), s32[]{:S(2)}) async-start(), calls=%async_computation.2 | async-start | bytes 3686400 | tf_op jit(solution)/shard_map/reduce_scatter | solution.py:323
  54.7 2.8 copy-start.8
  58.2 17.1 %copy-start.13 = (bf16[384,3840]{1,0:T(8,128)(2,1)S(1)}, bf16[384,3840]{1,0:T(8,128)(2,1)}, u32[]{:S(2)}) copy-start(bf16[384,3840]{1,0:T(8,128)(2,1)} %all-gather.2.cloned.1.call-done) | copy-start | bytes 8847364
  64.7 42.8 %collective-permute-start.2 = (bf16[2,384,512]{2,1,0:T(8,128)(2,1)}, bf16[2,384,512]{2,1,0:T(8,128)(2,1)}, u32[]{:S(2)}, u32[]{:S(2)}) collective-permute-start(bf16[2,384,512]{2,1,0:T(8,128)(2,1)} %pad_maximum_fusion.4), channel_id=1, source_target_pairs={{0,4},{4,8},{8,12},{12,16},{16,20},{20,24},{24,28},{28,32},{32,36}... | collective-permute-start | bytes 2359304 | tf_op jit(solution)/shard_map/ppermute | solution.py:21
  67.2 41.6 %collective-permute-start.1 = (bf16[2,384,512]{2,1,0:T(8,128)(2,1)}, bf16[2,384,512]{2,1,0:T(8,128)(2,1)}, u32[]{:S(2)}, u32[]{:S(2)}) collective-permute-start(bf16[2,384,512]{2,1,0:T(8,128)(2,1)} %pad_maximum_fusion.4), channel_id=1, source_target_pairs={{0,8},{4,12},{8,16},{12,20},{16,24},{20,28},{24,32},{28,36},{32,40... | collective-permute-start | bytes 2359304 | tf_op jit(solution)/shard_map/ppermute | solution.py:21
  71.0 39.0 %collective-permute-start = (bf16[2,384,512]{2,1,0:T(8,128)(2,1)}, bf16[2,384,512]{2,1,0:T(8,128)(2,1)}, u32[]{:S(2)}, u32[]{:S(2)}) collective-permute-start(bf16[2,384,512]{2,1,0:T(8,128)(2,1)} %pad_maximum_fusion.4), channel_id=1, source_target_pairs={{0,12},{4,16},{8,20},{12,24},{16,28},{20,32},{24,36},{28,40},{32,4... | collective-permute-start | bytes 2359304 | tf_op jit(solution)/shard_map/ppermute | solution.py:21
  93.1 2.0 copy-start.19
  106.3 4.8 %copy-start.15 = (bf16[384,512]{1,0:T(8,128)(2,1)S(1)}, bf16[384,512]{1,0:T(8,128)(2,1)}, u32[]{:S(2)}) copy-start(bf16[384,512]{1,0:T(8,128)(2,1)} %copy-done.14) | copy-start | bytes 1179652
  106.3 4.8 %copy-start.16 = (bf16[48,8,2,256]{3,1,2,0:T(8,128)(2,1)S(1)}, bf16[48,8,2,256]{3,1,2,0:T(8,128)(2,1)}, u32[]{:S(2)}) copy-start(bf16[48,8,2,256]{3,1,2,0:T(8,128)(2,1)} %copy.48) | copy-start | bytes 1179652
  106.3 94.2 %collective-permute-start.6 = (bf16[384,1920]{0,1:T(8,128)(2,1)}, bf16[384,1920]{0,1:T(8,128)(2,1)}, u32[]{:S(2)}, u32[]{:S(2)}) collective-permute-start(bf16[384,1920]{0,1:T(8,128)(2,1)} %bitcast.18), channel_id=1, source_target_pairs={{0,4},{4,0},{8,12},{12,8},{16,20},{20,16},{24,28},{28,24},{32,36},... | collective-permute-start | bytes 4423688 | tf_op jit(solution)/shard_map/ppermute | solution.py:230
  134.9 3.2 %copy-start.6 = (f32[1536,512]{1,0:T(8,128)S(1)}, f32[1536,512]{1,0:T(8,128)}, u32[]{:S(2)}) copy-start(f32[1536,512]{1,0:T(8,128)} %get-tuple-element.11) | copy-start | bytes 9437188
  138.5 4.3 %copy-start.23 = (f32[256]{0:T(256)S(1)}, f32[256]{0:T(256)}, u32[]{:S(2)}) copy-start(f32[256]{0:T(256)} %copy-done.22) | copy-start | bytes 3076
  138.6 19.8 %collective-permute-start.5 = (bf16[2,384,512]{2,1,0:T(8,128)(2,1)S(1)}, bf16[2,384,512]{2,1,0:T(8,128)(2,1)S(1)}, u32[]{:S(2)}, u32[]{:S(2)}) collective-permute-start(bf16[2,384,512]{2,1,0:T(8,128)(2,1)S(1)} %pad_maximum_fusion.7), channel_id=1, source_target_pairs={{12,0},{16,4},{20,8},{24,12},{28,16},{32,20},{36,24},{40,28},{44,3... | collective-permute-start | bytes 2359304 | tf_op jit(solution)/shard_map/ppermute | solution.py:21
  140.0 22.3 %collective-permute-start.4 = (bf16[2,384,512]{2,1,0:T(8,128)(2,1)S(1)}, bf16[2,384,512]{2,1,0:T(8,128)(2,1)S(1)}, u32[]{:S(2)}, u32[]{:S(2)}) collective-permute-start(bf16[2,384,512]{2,1,0:T(8,128)(2,1)S(1)} %pad_maximum_fusion.6), channel_id=1, source_target_pairs={{8,0},{12,4},{16,8},{20,12},{24,16},{28,20},{32,24},{36,28},{40,32... | collective-permute-start | bytes 2359304 | tf_op jit(solution)/shard_map/ppermute | solution.py:21
  141.4 20.9 %collective-permute-start.3 = (bf16[2,384,512]{2,1,0:T(8,128)(2,1)S(1)}, bf16[2,384,512]{2,1,0:T(8,128)(2,1)S(1)}, u32[]{:S(2)}, u32[]{:S(2)}) collective-permute-start(bf16[2,384,512]{2,1,0:T(8,128)(2,1)S(1)} %pad_maximum_fusion.5), channel_id=1, source_target_pairs={{4,0},{8,4},{12,8},{16,12},{20,16},{24,20},{28,24},{32,28},{36,32}... | collective-permute-start | bytes 2359304 | tf_op jit(solution)/shard_map/ppermute | solution.py:21
  144.4 2.3 copy-start.5
  144.4 2.3 copy-start.18
  162.7 3.8 %copy-start.21 = (f32[256]{0:T(256)S(1)}, f32[256]{0:T(256)}, u32[]{:S(2)}) copy-start(f32[256]{0:T(256)} %param.13) | copy-start | bytes 3076
  169.2 31.3 %collective-permute-start.7 = (bf16[384,2048]{1,0:T(8,128)(2,1)S(1)}, bf16[384,2048]{1,0:T(8,128)(2,1)S(1)}, u32[]{:S(2)}, u32[]{:S(2)}) collective-permute-start(bf16[384,2048]{1,0:T(8,128)(2,1)S(1)} %pad_maximum_fusion.3), channel_id=1, source_target_pairs={{0,4},{4,0},{8,12},{12,8},{16,20},{20,16},{24,28},{28,24},{32,36},... | collective-permute-start | bytes 4718600 | tf_op jit(solution)/shard_map/ppermute | solution.py:327
  190.0 6.3 %copy-start.7 = (bf16[3840,512]{1,0:T(8,128)(2,1)S(1)}, bf16[3840,512]{1,0:T(8,128)(2,1)}, u32[]{:S(2)}) copy-start(bf16[3840,512]{1,0:T(8,128)(2,1)} %param.10) | copy-start | bytes 11796484
  223.4 27.0 %collective-permute-start.14 = (bf16[4,120,512]{2,1,0:T(8,128)(2,1)S(1)}, bf16[4,120,512]{2,1,0:T(8,128)(2,1)S(1)}, u32[]{:S(2)}, u32[]{:S(2)}) collective-permute-start(bf16[4,120,512]{2,1,0:T(8,128)(2,1)S(1)} %fusion.12), channel_id=1, source_target_pairs={{8,0},{12,4},{16,8},{20,12},{24,16},{28,20},{0,24},{4,28},{40,32},... | collective-permute-start | bytes 1474568 | tf_op jit(solution)/shard_map/ppermute | solution.py:58
  244.0 14.2 %collective-permute-start.8 = (bf16[4,120,512]{2,1,0:T(8,128)(2,1)S(1)}, bf16[4,120,512]{2,1,0:T(8,128)(2,1)S(1)}, u32[]{:S(2)}, u32[]{:S(2)}) collective-permute-start(bf16[4,120,512]{2,1,0:T(8,128)(2,1)S(1)} %fusion.15), channel_id=1, source_target_pairs={{0,8},{4,12},{8,16},{12,20},{16,24},{20,28},{24,0},{28,4},{32,40},... | collective-permute-start | bytes 1474568 | tf_op jit(solution)/shard_map/ppermute | solution.py:55
  244.1 15.6 %copy-start.1 = (f32[4,4,120,512]{3,2,1,0:T(8,128)S(1)}, f32[4,4,120,512]{3,2,1,0:T(8,128)}, u32[]{:S(2)}) copy-start(f32[4,4,120,512]{3,2,1,0:T(8,128)} %get-tuple-element.14) | copy-start | bytes 11796484
  245.5 14.2 %collective-permute-start.20 = (bf16[4,120,512]{2,1,0:T(8,128)(2,1)S(1)}, bf16[4,120,512]{2,1,0:T(8,128)(2,1)S(1)}, u32[]{:S(2)}, u32[]{:S(2)}) collective-permute-start(bf16[4,120,512]{2,1,0:T(8,128)(2,1)S(1)} %fusion.13), channel_id=1, source_target_pairs={{0,32},{4,36},{8,40},{12,44},{16,48},{20,52},{24,56},{28,60},{32,6... | collective-permute-start | bytes 1474568 | tf_op jit(solution)/shard_map/ppermute | solution.py:55
  248.4 13.0 %copy-start = (f32[4,4,120,512]{3,2,1,0:T(8,128)S(1)}, f32[4,4,120,512]{3,2,1,0:T(8,128)}, u32[]{:S(2)}) copy-start(f32[4,4,120,512]{3,2,1,0:T(8,128)} %get-tuple-element.13) | copy-start | bytes 11796484
  248.4 13.0 %collective-permute-start.26 = (bf16[4,120,512]{2,1,0:T(8,128)(2,1)S(1)}, bf16[4,120,512]{2,1,0:T(8,128)(2,1)S(1)}, u32[]{:S(2)}, u32[]{:S(2)}) collective-permute-start(bf16[4,120,512]{2,1,0:T(8,128)(2,1)S(1)} %fusion.14), channel_id=1, source_target_pairs={{32,0},{36,4},{40,8},{44,12},{48,16},{52,20},{56,24},{60,28},{64,3... | collective-permute-start | bytes 1474568 | tf_op jit(solution)/shard_map/ppermute | solution.py:58
  251.8 12.8 %collective-permute-start.15 = (bf16[4,120,512]{2,1,0:T(8,128)(2,1)S(1)}, bf16[4,120,512]{2,1,0:T(8,128)(2,1)S(1)}, u32[]{:S(2)}, u32[]{:S(2)}) collective-permute-start(bf16[4,120,512]{2,1,0:T(8,128)(2,1)S(1)} %fusion.11), channel_id=1, source_target_pairs={{8,0},{12,4},{16,8},{20,12},{24,16},{28,20},{0,24},{4,28},{40,32},... | collective-permute-start | bytes 1474568 | tf_op jit(solution)/shard_map/ppermute | solution.py:58
  259.5 13.4 %copy-start.2 = (f32[4,4,120,512]{3,2,1,0:T(8,128)S(1)}, f32[4,4,120,512]{3,2,1,0:T(8,128)}, u32[]{:S(2)}) copy-start(f32[4,4,120,512]{3,2,1,0:T(8,128)} %get-tuple-element.16) | copy-start | bytes 11796484
  259.5 13.4 %collective-permute-start.9 = (bf16[4,120,512]{2,1,0:T(8,128)(2,1)S(1)}, bf16[4,120,512]{2,1,0:T(8,128)(2,1)S(1)}, u32[]{:S(2)}, u32[]{:S(2)}) collective-permute-start(bf16[4,120,512]{2,1,0:T(8,128)(2,1)S(1)} %fusion.5), channel_id=1, source_target_pairs={{0,8},{4,12},{8,16},{12,20},{16,24},{20,28},{24,0},{28,4},{32,40},... | collective-permute-start | bytes 1474568 | tf_op jit(solution)/shard_map/ppermute | solution.py:55
  259.8 13.4 %collective-permute-start.21 = (bf16[4,120,512]{2,1,0:T(8,128)(2,1)S(1)}, bf16[4,120,512]{2,1,0:T(8,128)(2,1)S(1)}, u32[]{:S(2)}, u32[]{:S(2)}) collective-permute-start(bf16[4,120,512]{2,1,0:T(8,128)(2,1)S(1)} %fusion.9), channel_id=1, source_target_pairs={{0,32},{4,36},{8,40},{12,44},{16,48},{20,52},{24,56},{28,60},{32,6... | collective-permute-start | bytes 1474568 | tf_op jit(solution)/shard_map/ppermute | solution.py:55
  261.6 13.4 %collective-permute-start.27 = (bf16[4,120,512]{2,1,0:T(8,128)(2,1)S(1)}, bf16[4,120,512]{2,1,0:T(8,128)(2,1)S(1)}, u32[]{:S(2)}, u32[]{:S(2)}) collective-permute-start(bf16[4,120,512]{2,1,0:T(8,128)(2,1)S(1)} %fusion.7), channel_id=1, source_target_pairs={{32,0},{36,4},{40,8},{44,12},{48,16},{52,20},{56,24},{60,28},{64,3... | collective-permute-start | bytes 1474568 | tf_op jit(solution)/shard_map/ppermute | solution.py:58
  266.0 12.6 %collective-permute-start.16 = (bf16[4,120,512]{2,1,0:T(8,128)(2,1)S(1)}, bf16[4,120,512]{2,1,0:T(8,128)(2,1)S(1)}, u32[]{:S(2)}, u32[]{:S(2)}) collective-permute-start(bf16[4,120,512]{2,1,0:T(8,128)(2,1)S(1)} %fusion.10), channel_id=1, source_target_pairs={{8,0},{12,4},{16,8},{20,12},{24,16},{28,20},{0,24},{4,28},{40,32},... | collective-permute-start | bytes 1474568 | tf_op jit(solution)/shard_map/ppermute | solution.py:58
  273.1 12.6 %collective-permute-start.10 = (bf16[4,120,512]{2,1,0:T(8,128)(2,1)S(1)}, bf16[4,120,512]{2,1,0:T(8,128)(2,1)S(1)}, u32[]{:S(2)}, u32[]{:S(2)}) collective-permute-start(bf16[4,120,512]{2,1,0:T(8,128)(2,1)S(1)} %fusion.4), channel_id=1, source_target_pairs={{0,8},{4,12},{8,16},{12,20},{16,24},{20,28},{24,0},{28,4},{32,40},... | collective-permute-start | bytes 1474568 | tf_op jit(solution)/shard_map/ppermute | solution.py:55
  273.4 14.2 %collective-permute-start.22 = (bf16[4,120,512]{2,1,0:T(8,128)(2,1)S(1)}, bf16[4,120,512]{2,1,0:T(8,128)(2,1)S(1)}, u32[]{:S(2)}, u32[]{:S(2)}) collective-permute-start(bf16[4,120,512]{2,1,0:T(8,128)(2,1)S(1)} %fusion.8), channel_id=1, source_target_pairs={{0,32},{4,36},{8,40},{12,44},{16,48},{20,52},{24,56},{28,60},{32,6... | collective-permute-start | bytes 1474568 | tf_op jit(solution)/shard_map/ppermute | solution.py:55
  275.1 12.7 %collective-permute-start.28 = (bf16[4,120,512]{2,1,0:T(8,128)(2,1)S(1)}, bf16[4,120,512]{2,1,0:T(8,128)(2,1)S(1)}, u32[]{:S(2)}, u32[]{:S(2)}) collective-permute-start(bf16[4,120,512]{2,1,0:T(8,128)(2,1)S(1)} %fusion.6), channel_id=1, source_target_pairs={{32,0},{36,4},{40,8},{44,12},{48,16},{52,20},{56,24},{60,28},{64,3... | collective-permute-start | bytes 1474568 | tf_op jit(solution)/shard_map/ppermute | solution.py:58
  279.9 11.4 %collective-permute-start.17 = (bf16[120,512]{1,0:T(8,128)(2,1)S(1)}, bf16[120,512]{1,0:T(8,128)(2,1)S(1)}, u32[]{:S(2)}, u32[]{:S(2)}) collective-permute-start(bf16[120,512]{1,0:T(8,128)(2,1)S(1)} %fusion.30), channel_id=1, source_target_pairs={{32,0},{36,4},{40,8},{44,12},{48,16},{52,20},{56,24},{60,28},{64,3... | collective-permute-start | bytes 368648 | tf_op jit(solution)/shard_map/ppermute | solution.py:58
  285.9 8.2 %collective-permute-start.11 = (bf16[120,512]{1,0:T(8,128)(2,1)S(1)}, bf16[120,512]{1,0:T(8,128)(2,1)S(1)}, u32[]{:S(2)}, u32[]{:S(2)}) collective-permute-start(bf16[120,512]{1,0:T(8,128)(2,1)S(1)} %fusion.29), channel_id=1, source_target_pairs={{0,32},{4,36},{8,40},{12,44},{16,48},{20,52},{24,56},{28,60},{32,6... | collective-permute-start | bytes 368648 | tf_op jit(solution)/shard_map/ppermute | solution.py:55
  287.7 6.5 %collective-permute-start.23 = (bf16[120,512]{1,0:T(8,128)(2,1)S(1)}, bf16[120,512]{1,0:T(8,128)(2,1)S(1)}, u32[]{:S(2)}, u32[]{:S(2)}) collective-permute-start(bf16[120,512]{1,0:T(8,128)(2,1)S(1)} %fusion.31), channel_id=1, source_target_pairs={{0,8},{4,12},{8,16},{12,20},{16,24},{20,28},{24,0},{28,4},{32,40},... | collective-permute-start | bytes 368648 | tf_op jit(solution)/shard_map/ppermute | solution.py:55
  288.0 6.3 %collective-permute-start.29 = (bf16[120,512]{1,0:T(8,128)(2,1)S(1)}, bf16[120,512]{1,0:T(8,128)(2,1)S(1)}, u32[]{:S(2)}, u32[]{:S(2)}) collective-permute-start(bf16[120,512]{1,0:T(8,128)(2,1)S(1)} %fusion.32), channel_id=1, source_target_pairs={{8,0},{12,4},{16,8},{20,12},{24,16},{28,20},{0,24},{4,28},{40,32},... | collective-permute-start | bytes 368648 | tf_op jit(solution)/shard_map/ppermute | solution.py:58
  291.3 6.6 %collective-permute-start.18 = (bf16[120,512]{1,0:T(8,128)(2,1)S(1)}, bf16[120,512]{1,0:T(8,128)(2,1)S(1)}, u32[]{:S(2)}, u32[]{:S(2)}) collective-permute-start(bf16[120,512]{1,0:T(8,128)(2,1)S(1)} %fusion.25), channel_id=1, source_target_pairs={{32,0},{36,4},{40,8},{44,12},{48,16},{52,20},{56,24},{60,28},{64,3... | collective-permute-start | bytes 368648 | tf_op jit(solution)/shard_map/ppermute | solution.py:58
  294.1 7.2 %collective-permute-start.12 = (bf16[120,512]{1,0:T(8,128)(2,1)S(1)}, bf16[120,512]{1,0:T(8,128)(2,1)S(1)}, u32[]{:S(2)}, u32[]{:S(2)}) collective-permute-start(bf16[120,512]{1,0:T(8,128)(2,1)S(1)} %fusion.28), channel_id=1, source_target_pairs={{0,32},{4,36},{8,40},{12,44},{16,48},{20,52},{24,56},{28,60},{32,6... | collective-permute-start | bytes 368648 | tf_op jit(solution)/shard_map/ppermute | solution.py:55
  294.2 7.2 %collective-permute-start.24 = (bf16[120,512]{1,0:T(8,128)(2,1)S(1)}, bf16[120,512]{1,0:T(8,128)(2,1)S(1)}, u32[]{:S(2)}, u32[]{:S(2)}) collective-permute-start(bf16[120,512]{1,0:T(8,128)(2,1)S(1)} %fusion.22), channel_id=1, source_target_pairs={{0,8},{4,12},{8,16},{12,20},{16,24},{20,28},{24,0},{28,4},{32,40},... | collective-permute-start | bytes 368648 | tf_op jit(solution)/shard_map/ppermute | solution.py:55
  294.4 7.1 %collective-permute-start.30 = (bf16[120,512]{1,0:T(8,128)(2,1)S(1)}, bf16[120,512]{1,0:T(8,128)(2,1)S(1)}, u32[]{:S(2)}, u32[]{:S(2)}) collective-permute-start(bf16[120,512]{1,0:T(8,128)(2,1)S(1)} %fusion.19), channel_id=1, source_target_pairs={{8,0},{12,4},{16,8},{20,12},{24,16},{28,20},{0,24},{4,28},{40,32},... | collective-permute-start | bytes 368648 | tf_op jit(solution)/shard_map/ppermute | solution.py:58
  297.9 7.3 %collective-permute-start.19 = (bf16[120,512]{1,0:T(8,128)(2,1)S(1)}, bf16[120,512]{1,0:T(8,128)(2,1)S(1)}, u32[]{:S(2)}, u32[]{:S(2)}) collective-permute-start(bf16[120,512]{1,0:T(8,128)(2,1)S(1)} %fusion.24), channel_id=1, source_target_pairs={{32,0},{36,4},{40,8},{44,12},{48,16},{52,20},{56,24},{60,28},{64,3... | collective-permute-start | bytes 368648 | tf_op jit(solution)/shard_map/ppermute | solution.py:58
  301.3 6.2 %collective-permute-start.13 = (bf16[120,512]{1,0:T(8,128)(2,1)S(1)}, bf16[120,512]{1,0:T(8,128)(2,1)S(1)}, u32[]{:S(2)}, u32[]{:S(2)}) collective-permute-start(bf16[120,512]{1,0:T(8,128)(2,1)S(1)} %fusion.27), channel_id=1, source_target_pairs={{0,32},{4,36},{8,40},{12,44},{16,48},{20,52},{24,56},{28,60},{32,6... | collective-permute-start | bytes 368648 | tf_op jit(solution)/shard_map/ppermute | solution.py:55
  301.4 6.2 %collective-permute-start.25 = (bf16[120,512]{1,0:T(8,128)(2,1)S(1)}, bf16[120,512]{1,0:T(8,128)(2,1)S(1)}, u32[]{:S(2)}, u32[]{:S(2)}) collective-permute-start(bf16[120,512]{1,0:T(8,128)(2,1)S(1)} %fusion.21), channel_id=1, source_target_pairs={{0,8},{4,12},{8,16},{12,20},{16,24},{20,28},{24,0},{28,4},{32,40},... | collective-permute-start | bytes 368648 | tf_op jit(solution)/shard_map/ppermute | solution.py:55
  301.6 7.4 %collective-permute-start.31 = (bf16[120,512]{1,0:T(8,128)(2,1)S(1)}, bf16[120,512]{1,0:T(8,128)(2,1)S(1)}, u32[]{:S(2)}, u32[]{:S(2)}) collective-permute-start(bf16[120,512]{1,0:T(8,128)(2,1)S(1)} %fusion.18), channel_id=1, source_target_pairs={{8,0},{12,4},{16,8},{20,12},{24,16},{28,20},{0,24},{4,28},{40,32},... | collective-permute-start | bytes 368648 | tf_op jit(solution)/shard_map/ppermute | solution.py:58
  (11 other events, 15.0 us)
Sparse Core Ops, SparseCore 0:
  9.6 40.2 all-gather.1
  242.8 34.0 reduce-scatter.1
where the time goes:
time: 322 us; the launch traced here: 317 us
  starting transfers between devices  81.4 us (25%)
  waiting for transfers between devices  66.5 us (21%)
  local copies, waits for them, and re-layouts  58 us (18%)
  matrix products  49.7 us (15%)
  other arithmetic  31.1 us (10%)
  between operations  15.4 us (5%)
  Pallas kernels  14.7 us (5%)
    ppermute x12, starting transfers between devices, ring_reduce_scatter(): lax.ppermute(down.astype(jnp.bfloat16), 'ctx', backward).astype(jnp.float32)  43.5 us
    all_gather x1, waiting for transfers between devices, on_device(): gathered = lax.all_gather(tokens, 'head', axis=0, tiled=True)  36.9 us
    dot_general x2, matrix products, rounded_term(): lax.dot_general(rows, columns, (((0,), (0,)), ((), ())), preferred_elemen...  15.2 us
    ppermute x1, starting transfers between devices, on_device(): partner_columns = lax.ppermute(grad_columns, 'ctx', partner)  15 us
    pallas_call x1, Pallas kernels, fused_attention(): pl.pallas_call(attention_body, grid=(groups,), in_specs=[pl.BlockSpec((ro...  14.7 us
    ppermute x6, starting transfers between devices, passed_along(): return lax.ppermute(block, axis, route)  14.6 us
    ppermute x12, waiting for transfers between devices, ring_reduce_scatter(): lax.ppermute(up.astype(jnp.bfloat16), 'ctx', forward).astype(jnp.float32)  14.1 us
    ppermute x6, waiting for transfers between devices, passed_along(): return lax.ppermute(block, axis, route)  13.7 us
  transfers between devices with their start and end apart: 34, of which 13 were waited for; matrix products, arithmetic and copies ran while one was open for 31% of the time, Pallas kernels for 5%

commit v1 on v0

--- a/solution.py
+++ b/solution.py
@@ -76,17 +76,16 @@
     )
 
 
-def torus_reduce_scatter(pair_sum, my_rank, rank_count):
+def torus_reduce_scatter(first, second, my_rank, rank_count):
     z_chips = rank_count // (CORES * Y_CHIPS)
-    rows, columns = pair_sum.shape
+    rows = first.shape[0]
     y_pos = (my_rank // CORES) % Y_CHIPS
     z_pos = my_rank // (CORES * Y_CHIPS)
-    grid = pair_sum.reshape(z_chips, Y_CHIPS, rows // (z_chips * Y_CHIPS), columns)
+    per_rank = rows // (z_chips * Y_CHIPS)
+    first = first.reshape(z_chips, Y_CHIPS, per_rank, first.shape[-1])
+    second = second.reshape(z_chips, Y_CHIPS, per_rank, second.shape[-1])
     y_forward, y_backward = ring_pairs(rank_count, True)
     z_forward, z_backward = ring_pairs(rank_count, False)
-    half = columns // 2
-    first = grid[..., :half]
-    second = grid[..., half:]
     first = ring_reduce_scatter(first, 1, y_pos, y_forward, y_backward)
     first = ring_reduce_scatter(first, 0, z_pos, z_forward, z_backward)
     second = ring_reduce_scatter(second, 0, z_pos, z_forward, z_backward)
@@ -315,6 +314,19 @@
         .astype(jnp.bfloat16)
         .reshape(row_count, groups * head_width)
     )
+    query_sum = rounded_term(my_rows, query_raw_grad) + rounded_term(
+        partner_rows, lax.ppermute(query_raw_grad, "ctx", partner)
+    )
+    kv_columns = jnp.concatenate([key_raw_grad, value_grads], axis=1)
+    kv_sum = rounded_term(my_rows, kv_columns) + rounded_term(
+        partner_rows, lax.ppermute(kv_columns, "ctx", partner)
+    )
+    kv_sum, query_raw_grad, key_raw_grad, value_grads = lax.optimization_barrier(
+        (kv_sum, query_raw_grad, key_raw_grad, value_grads)
+    )
+    summed = torus_reduce_scatter(query_sum, kv_sum, my_rank, rank_count).astype(
+        jnp.bfloat16
+    )
     input_terms = (
         jnp.dot(query_raw_grad, w_query.T, preferred_element_type=jnp.float32)
         + jnp.dot(key_raw_grad, w_key.T, preferred_element_type=jnp.float32)
@@ -323,10 +335,6 @@
     input_grad = lax.psum_scatter(
         input_terms.astype(jnp.bfloat16), "head", scatter_dimension=0, tiled=True
     )
-    grad_columns = jnp.concatenate([query_raw_grad, key_raw_grad, value_grads], axis=1)
-    partner_columns = lax.ppermute(grad_columns, "ctx", partner)
-    pair_sum = rounded_term(my_rows, grad_columns) + rounded_term(partner_rows, partner_columns)
-    summed = torus_reduce_scatter(pair_sum, my_rank, rank_count).astype(jnp.bfloat16)
     query_cols = head_count * head_width
     key_cols = groups * head_width
     return (

time: 322 us -> 325 us (level)
  waiting for transfers between devices: 66.5 us -> 103 us
  starting transfers between devices: 81.4 us -> 68.1 us
  local copies, waits for them, and re-layouts: 58 us -> 45.8 us
  matrix products: 49.7 us -> 40.6 us
    ppermute x6, waiting for transfers between devices: 13.7 us -> 27.4 us  [passed_along(): return lax.ppermute(block, axis, route)]
    ppermute x12, starting transfers between devices: 43.5 us -> 30.5 us  [ring_reduce_scatter(): lax.ppermute(down.astype(jnp.bfloat16), 'ctx', backward).astype(jnp.float32)]
    ppermute x12, waiting for transfers between devices: 1.02 us -> 13.6 us  [ring_reduce_scatter(): lax.ppermute(down.astype(jnp.bfloat16), 'ctx', backward).astype(jnp.float32)]
    ppermute x12, waiting for transfers between devices: 14.1 us -> 24.5 us  [ring_reduce_scatter(): lax.ppermute(up.astype(jnp.bfloat16), 'ctx', forward).astype(jnp.float32)]
    slice x1 -> x2, local copies, waits for them, and re-layouts: 12.6 us -> 4.19 us  [own(): piece = lax.slice_in_dim(parts, low, low + half, axis=parts.ndim - 1)]
    ppermute x1 -> x2, starting transfers between devices: 15 us -> 9.92 us  [the longest x1 6.93 us: on_device(): lax.ppermute(kv_columns, 'ctx', partner)]
    ppermute x12, starting transfers between devices: 6.99 us -> 11.9 us  [ring_reduce_scatter(): lax.ppermute(up.astype(jnp.bfloat16), 'ctx', forward).astype(jnp.float32)]
    dot_general x1, matrix products: 7.18 us -> 3.33 us  [on_device(): jnp.dot(value_grads, w_value.T, preferred_element_type=jnp.float32)]
  transfers between devices with their start and end apart: 34 -> 35, of which waited for: 13 -> 17; matrix products, arithmetic and copies ran while one was open for 31% -> 30% of each run, Pallas kernels for 5% -> 5%
where the time goes in v1:
time: 325 us; the launch traced here: 320 us
  waiting for transfers between devices  103 us (32%)
  starting transfers between devices  68.1 us (21%)
  local copies, waits for them, and re-layouts  45.8 us (14%)
  matrix products  40.6 us (12%)
  other arithmetic  31.9 us (10%)
  between operations  15.5 us (5%)
  Pallas kernels  14.7 us (5%)
    all_gather x1, waiting for transfers between devices, on_device(): gathered = lax.all_gather(tokens, 'head', axis=0, tiled=True)  36.9 us
    ppermute x12, starting transfers between devices, ring_reduce_scatter(): lax.ppermute(down.astype(jnp.bfloat16), 'ctx', backward).astype(jnp.float32)  30.5 us
    ppermute x6, waiting for transfers between devices, passed_along(): return lax.ppermute(block, axis, route)  27.4 us
    ppermute x12, waiting for transfers between devices, ring_reduce_scatter(): lax.ppermute(up.astype(jnp.bfloat16), 'ctx', forward).astype(jnp.float32)  24.5 us
    ppermute x6, starting transfers between devices, passed_along(): return lax.ppermute(block, axis, route)  15.6 us
    pallas_call x1, Pallas kernels, fused_attention(): pl.pallas_call(attention_body, grid=(groups,), in_specs=[pl.BlockSpec((ro...  14.7 us
    unnamed x88, local copies, waits for them, and re-layouts  14.1 us
    ppermute x12, waiting for transfers between devices, ring_reduce_scatter(): lax.ppermute(down.astype(jnp.bfloat16), 'ctx', backward).astype(jnp.float32)  13.6 us
  transfers between devices with their start and end apart: 35, of which 17 were waited for; matrix products, arithmetic and copies ran while one was open for 30% of the time, Pallas kernels for 5%

profile of v1, /device:TPU:0, one launch (start us, length us, event | category | flops | bytes accessed | tf_op | source)
XLA Modules:
  0.0 319.6 jit_solution(7315351325742509815)
XLA Ops:
  13.1 36.9 %all-gather.2.cloned.1.call-done = bf16[384,3840]{1,0:T(8,128)(2,1)} async-done(((bf16[96,3840]{1,0:T(8,128)(2,1)}), bf16[384,3840]{1,0:T(8,128)(2,1)}) %all-gather.2.cloned.1.call-update) | async-done | bytes 2949136 | tf_op jit(solution)/shard_map/all_gather | solution.py:217
  50.0 4.7 %fusion.37 = f32[384,512]{1,0:T(8,128)S(1)} fusion(bf16[384,3840]{1,0:T(8,128)(2,1)} %all-gather.2.cloned.1.call-done, bf16[3840,512]{1,0:T(8,128)(2,1)} %param.10), kind=kOutput, calls=%fused_computation.133 | convolution fusion | flops 1509949440 | bytes 7667712 | tf_op jit(solution)/shard_map/dot_general | solution.py:236
  58.2 4.8 %convolution_convert_fusion = bf16[384,512]{1,0:T(8,128)(2,1)S(1)} fusion(bf16[384,3840]{1,0:T(8,128)(2,1)} %all-gather.2.cloned.1.call-done, bf16[3840,512]{1,0:T(8,128)(2,1)} %param.11), kind=kOutput, calls=%fused_computation.17 | convolution fusion | flops 1510146048 | bytes 7274496 | tf_op jit(solution)/shard_map/dot_general | solution.py:239
  64.0 3.6 %collective-permute-start = (bf16[2,384,512]{2,1,0:T(8,128)(2,1)}, bf16[2,384,512]{2,1,0:T(8,128)(2,1)}, u32[]{:S(2)}, u32[]{:S(2)}) collective-permute-start(bf16[2,384,512]{2,1,0:T(8,128)(2,1)} %pad_maximum_fusion.3), channel_id=1, source_target_pairs={{0,12},{4,16},{8,20},{12,24},{16,28},{20,32},{24,36},{28,40},{32,4... | collective-permute-start | bytes 2359304 | tf_op jit(solution)/shard_map/ppermute | solution.py:21
  67.6 4.3 %collective-permute-start.1 = (bf16[2,384,512]{2,1,0:T(8,128)(2,1)}, bf16[2,384,512]{2,1,0:T(8,128)(2,1)}, u32[]{:S(2)}, u32[]{:S(2)}) collective-permute-start(bf16[2,384,512]{2,1,0:T(8,128)(2,1)} %pad_maximum_fusion.3), channel_id=1, source_target_pairs={{0,8},{4,12},{8,16},{12,20},{16,24},{20,28},{24,32},{28,36},{32,40... | collective-permute-start | bytes 2359304 | tf_op jit(solution)/shard_map/ppermute | solution.py:21
  71.9 3.6 %collective-permute-start.2 = (bf16[2,384,512]{2,1,0:T(8,128)(2,1)}, bf16[2,384,512]{2,1,0:T(8,128)(2,1)}, u32[]{:S(2)}, u32[]{:S(2)}) collective-permute-start(bf16[2,384,512]{2,1,0:T(8,128)(2,1)} %pad_maximum_fusion.3), channel_id=1, source_target_pairs={{0,4},{4,8},{8,12},{12,16},{16,20},{20,24},{24,28},{28,32},{32,36}... | collective-permute-start | bytes 2359304 | tf_op jit(solution)/shard_map/ppermute | solution.py:21
  76.3 5.5 %fusion.36 = f32[384,1024]{1,0:T(8,128)S(1)} fusion(bf16[384,3840]{1,0:T(8,128)(2,1)S(1)} %copy-done.21, bf16[3840,1024]{1,0:T(8,128)(2,1)} %param.9), kind=kOutput, calls=%fused_computation.132 | convolution fusion | flops 3019898880 | bytes 12386304 | tf_op jit(solution)/shard_map/dot_general | solution.py:233
  97.4 4.5 %copy.38 = bf16[384,3840]{0,1:T(8,128)(2,1)} copy(bf16[384,3840]{1,0:T(8,128)(2,1)} %all-gather.2.cloned.1.call-done) | data formatting | bytes 5898240 | tf_op jit(solution)/shard_map/all_gather | solution.py:217
  101.9 3.7 %constant_dynamic-slice_fusion = (bf16[384,4,4,1,120]{0,4,3,2,1:T(8,128)(2,1)}, bf16[384,4,4,1,120]{0,4,3,2,1:T(8,128)(2,1)}) fusion(bf16[384,4,4,2,120]{0,4,3,2,1:T(8,128)(2,1)} %bitcast.207, s32[]{:T(128)S(6)} %select_n.174, s32[]{:T(128)S(6)} %select_n.173), kind=kLoop, calls=%fused_computation.119 | loop fusion | bytes 5898248 | tf_op jit(solution)/shard_map/jit(dynamic_index_in_dim)/dynamic_slice | solution.py:68
  109.4 1.8 pad_maximum_fusion
  111.2 14.7 %shard_map.119 = (bf16[384,1024]{1,0:T(8,128)(2,1)}, f32[384,1024]{1,0:T(8,128)}, f32[1536,512]{1,0:T(8,128)}, f32[1536,512]{1,0:T(8,128)}) custom-call(bf16[384,1024]{1,0:T(8,128)(2,1)} %bitcast.230, bf16[1536,512]{1,0:T(8,128)(2,1)} %get-tuple-element.59.k_ref, bf16[1536,512]{1,0:T(8,128)(2,1)} %get-tuple-element.60.v_ref, bf16[384,1024]{1,0:T(8,128)(2,1)} %do_ref.1, ...), custom_call_target="tpu_custom_call" | custom-call | flops 7247757312 | bytes 13369344 | tf_op jit(solution)/shard_map/pallas_call | solution.py:141
  125.9 2.9 reshape.168
  128.8 1.8 multiply_add_fusion
  140.4 1.8 subtract_convert_fusion
  142.2 3.0 collective-permute-start.8
  145.2 5.2 %fusion.39 = bf16[1920,1024]{1,0:T(8,128)(2,1)} fusion(bf16[384,1920]{0,1:T(8,128)(2,1)S(1)} %bitcast.228, bf16[384,1024]{1,0:T(8,128)(2,1)} %subtract_convert_fusion), kind=kOutput, calls=%fused_computation.135 | convolution fusion | flops 1509949440 | bytes 6193152 | tf_op jit(solution)/shard_map/dot_general | solution.py:73
  150.5 25.6 %collective-permute-done.4 = bf16[2,384,512]{2,1,0:T(8,128)(2,1)S(1)} collective-permute-done((bf16[2,384,512]{2,1,0:T(8,128)(2,1)S(1)}, bf16[2,384,512]{2,1,0:T(8,128)(2,1)S(1)}, u32[]{:S(2)}, u32[]{:S(2)}) %collective-permute-start.4) | collective-permute-done | bytes 786464 | tf_op jit(solution)/shard_map/ppermute | solution.py:21
  176.1 1.8 collective-permute-done.5
  185.6 3.3 %convert_add_fusion = f32[1920,1024]{1,0:T(8,128)S(1)} fusion(bf16[1920,1024]{1,0:T(8,128)(2,1)S(1)} %copy-done.7, bf16[384,1920]{0,1:T(8,128)(2,1)S(1)} %collective-permute-done.6, bf16[384,1024]{1,0:T(8,128)(2,1)} %collective-permute-done.8), kind=kOutput, calls=%fused_computation | convolution fusion | flops 1517813760 | bytes 14057472 | tf_op jit(solution)/shard_map/dot_general | solution.py:73
  190.4 3.3 %collective-permute-start.9 = (bf16[4,120,512]{2,1,0:T(8,128)(2,1)S(1)}, bf16[4,120,512]{2,1,0:T(8,128)(2,1)S(1)}, u32[]{:S(2)}, u32[]{:S(2)}) collective-permute-start(bf16[4,120,512]{2,1,0:T(8,128)(2,1)S(1)} %fusion.14), channel_id=1, source_target_pairs={{0,8},{4,12},{8,16},{12,20},{16,24},{20,28},{24,0},{28,4},{32,40},... | collective-permute-start | bytes 1474568 | tf_op jit(solution)/shard_map/ppermute | solution.py:55
  194.4 6.9 %collective-permute-start.7 = (bf16[384,1024]{1,0:T(8,128)(2,1)S(1)}, bf16[384,1024]{1,0:T(8,128)(2,1)S(1)}, u32[]{:S(2)}, u32[]{:S(2)}) collective-permute-start(bf16[384,1024]{1,0:T(8,128)(2,1)S(1)} %pad_maximum_fusion.8), channel_id=1, source_target_pairs={{0,4},{4,0},{8,12},{12,8},{16,20},{20,16},{24,28},{28,24},{32,36},... | collective-permute-start | bytes 2359304 | tf_op jit(solution)/shard_map/ppermute | solution.py:322
  201.4 3.4 %collective-permute-start.15 = (bf16[4,120,512]{2,1,0:T(8,128)(2,1)S(1)}, bf16[4,120,512]{2,1,0:T(8,128)(2,1)S(1)}, u32[]{:S(2)}, u32[]{:S(2)}) collective-permute-start(bf16[4,120,512]{2,1,0:T(8,128)(2,1)S(1)} %fusion.15), channel_id=1, source_target_pairs={{8,0},{12,4},{16,8},{20,12},{24,16},{28,20},{0,24},{4,28},{40,32},... | collective-permute-start | bytes 1474568 | tf_op jit(solution)/shard_map/ppermute | solution.py:58
  204.7 2.2 fusion.33
  207.0 6.9 %collective-permute-done.9 = bf16[4,120,512]{2,1,0:T(8,128)(2,1)S(1)} collective-permute-done((bf16[4,120,512]{2,1,0:T(8,128)(2,1)S(1)}, bf16[4,120,512]{2,1,0:T(8,128)(2,1)S(1)}, u32[]{:S(2)}, u32[]{:S(2)}) %collective-permute-start.9) | collective-permute-done | bytes 491552 | tf_op jit(solution)/shard_map/ppermute | solution.py:55
  216.8 4.1 %collective-permute-start.16 = (bf16[4,120,512]{2,1,0:T(8,128)(2,1)}, bf16[4,120,512]{2,1,0:T(8,128)(2,1)}, u32[]{:S(2)}, u32[]{:S(2)}) collective-permute-start(bf16[4,120,512]{2,1,0:T(8,128)(2,1)} %fusion.5), channel_id=1, source_target_pairs={{8,0},{12,4},{16,8},{20,12},{24,16},{28,20},{0,24},{4,28},{40,32},... | collective-permute-start | bytes 1474568 | tf_op jit(solution)/shard_map/ppermute | solution.py:58
  220.9 2.2 convert_add_fusion.1
  223.1 2.9 fusion.34
  227.0 7.5 %fusion.38 = f32[384,3840]{1,0:T(8,128)S(1)} fusion(bf16[384,1024]{1,0:T(8,128)(2,1)} %subtract_convert_fusion, bf16[3840,1024]{1,0:T(8,128)(2,1)} %param.9), kind=kOutput, calls=%fused_computation.134 | convolution fusion | flops 3019898880 | bytes 14548992 | tf_op jit(solution)/shard_map/dot_general | solution.py:331
  234.5 1.7 convolution_add_fusion.1
  236.6 3.3 %fusion = bf16[384,3840]{1,0:T(8,128)(2,1)} fusion(f32[384,3840]{1,0:T(8,128)S(1)} %convolution_add_fusion.1, bf16[384,512]{1,0:T(8,128)(2,1)S(1)} %fusion.16, bf16[3840,512]{1,0:T(8,128)(2,1)S(1)} %copy-done.16), kind=kOutput, calls=%fused_computation.4 | convolution fusion | flops 1512898560 | bytes 13172736 | tf_op jit(solution)/shard_map/dot_general | solution.py:333
  245.7 3.3 %collective-permute-start.17 = (bf16[4,120,512]{2,1,0:T(8,128)(2,1)S(1)}, bf16[4,120,512]{2,1,0:T(8,128)(2,1)S(1)}, u32[]{:S(2)}, u32[]{:S(2)}) collective-permute-start(bf16[4,120,512]{2,1,0:T(8,128)(2,1)S(1)} %fusion.4), channel_id=1, source_target_pairs={{8,0},{12,4},{16,8},{20,12},{24,16},{28,20},{0,24},{4,28},{40,32},... | collective-permute-start | bytes 1474568 | tf_op jit(solution)/shard_map/ppermute | solution.py:58
  250.3 2.0 collective-permute-start.28
  252.3 1.8 collective-permute-done.21
  254.9 2.3 collective-permute-done.11
  258.6 1.7 collective-permute-start.12
  263.4 5.8 %collective-permute-done.12 = bf16[120,512]{1,0:T(8,128)(2,1)S(1)} collective-permute-done((bf16[120,512]{1,0:T(8,128)(2,1)S(1)}, bf16[120,512]{1,0:T(8,128)(2,1)S(1)}, u32[]{:S(2)}, u32[]{:S(2)}) %collective-permute-start.12) | collective-permute-done | bytes 122912 | tf_op jit(solution)/shard_map/ppermute | solution.py:55
  269.3 3.4 %collective-permute-start.19 = (bf16[120,512]{1,0:T(8,128)(2,1)S(1)}, bf16[120,512]{1,0:T(8,128)(2,1)S(1)}, u32[]{:S(2)}, u32[]{:S(2)}) collective-permute-start(bf16[120,512]{1,0:T(8,128)(2,1)S(1)} %fusion.25), channel_id=1, source_target_pairs={{32,0},{36,4},{40,8},{44,12},{48,16},{52,20},{56,24},{60,28},{64,3... | collective-permute-start | bytes 368648 | tf_op jit(solution)/shard_map/ppermute | solution.py:58
  272.8 2.6 collective-permute-done.13
  275.5 3.6 %collective-permute-start.20 = (bf16[120,512]{1,0:T(8,128)(2,1)S(1)}, bf16[120,512]{1,0:T(8,128)(2,1)S(1)}, u32[]{:S(2)}, u32[]{:S(2)}) collective-permute-start(bf16[120,512]{1,0:T(8,128)(2,1)S(1)} %fusion.24), channel_id=1, source_target_pairs={{32,0},{36,4},{40,8},{44,12},{48,16},{52,20},{56,24},{60,28},{64,3... | collective-permute-start | bytes 368648 | tf_op jit(solution)/shard_map/ppermute | solution.py:58
  279.5 2.1 collective-permute-start.23
  283.7 5.7 %collective-permute-done.29 = bf16[4,120,512]{2,1,0:T(8,128)(2,1)S(1)} collective-permute-done((bf16[4,120,512]{2,1,0:T(8,128)(2,1)S(1)}, bf16[4,120,512]{2,1,0:T(8,128)(2,1)S(1)}, u32[]{:S(2)}, u32[]{:S(2)}) %collective-permute-start.29) | collective-permute-done | bytes 491552 | tf_op jit(solution)/shard_map/ppermute | solution.py:58
  289.5 2.2 collective-permute-start.30
  293.6 2.1 collective-permute-done.30
  295.7 2.5 collective-permute-start.31
  299.6 2.5 collective-permute-done.31
  302.1 3.5 %collective-permute-start.32 = (bf16[120,512]{1,0:T(8,128)(2,1)S(1)}, bf16[120,512]{1,0:T(8,128)(2,1)S(1)}, u32[]{:S(2)}, u32[]{:S(2)}) collective-permute-start(bf16[120,512]{1,0:T(8,128)(2,1)S(1)} %fusion.18), channel_id=1, source_target_pairs={{8,0},{12,4},{16,8},{20,12},{24,16},{28,20},{0,24},{4,28},{40,32},... | collective-permute-start | bytes 368648 | tf_op jit(solution)/shard_map/ppermute | solution.py:58
  305.9 2.2 collective-permute-done.32
  308.7 3.2 %collective-permute-done.26 = bf16[120,512]{1,0:T(8,128)(2,1)S(1)} collective-permute-done((bf16[120,512]{1,0:T(8,128)(2,1)S(1)}, bf16[120,512]{1,0:T(8,128)(2,1)S(1)}, u32[]{:S(2)}, u32[]{:S(2)}) %collective-permute-start.26) | collective-permute-done | bytes 122912 | tf_op jit(solution)/shard_map/ppermute | solution.py:55
  (218 shorter events, 73.7 us)
Async XLA Ops:
  7.2 42.8 %all-gather.2.cloned.1.call-start = ((), (), s32[]{:S(2)}) async-start(), calls=%async_computation.1 | async-start | bytes 3686400 | tf_op jit(solution)/shard_map/all_gather | solution.py:217
  7.9 304.7 %reduce-scatter.2.cloned.1.call-start = ((), (), s32[]{:S(2)}) async-start(), calls=%async_computation.2 | async-start | bytes 3686400 | tf_op jit(solution)/shard_map/reduce_scatter | solution.py:335
  56.6 6.4 %copy-start.23 = (f32[384,2]{1,0:T(8,128)}, f32[384,2]{1,0:T(8,128)S(1)}, u32[]{:S(2)}) copy-start(f32[384,2]{1,0:T(8,128)S(1)} %copy.36) | copy-start | bytes 9220
  58.2 18.2 %copy-start.21 = (bf16[384,3840]{1,0:T(8,128)(2,1)S(1)}, bf16[384,3840]{1,0:T(8,128)(2,1)}, u32[]{:S(2)}) copy-start(bf16[384,3840]{1,0:T(8,128)(2,1)} %all-gather.2.cloned.1.call-done) | copy-start | bytes 8847364
  63.0 13.3 %copy-start.25 = (bf16[384,512]{1,0:T(8,128)(2,1)}, bf16[384,512]{1,0:T(8,128)(2,1)S(1)}, u32[]{:S(2)}) copy-start(bf16[384,512]{1,0:T(8,128)(2,1)S(1)} %convolution_convert_fusion) | copy-start | bytes 1179652
  64.0 41.7 %collective-permute-start = (bf16[2,384,512]{2,1,0:T(8,128)(2,1)}, bf16[2,384,512]{2,1,0:T(8,128)(2,1)}, u32[]{:S(2)}, u32[]{:S(2)}) collective-permute-start(bf16[2,384,512]{2,1,0:T(8,128)(2,1)} %pad_maximum_fusion.3), channel_id=1, source_target_pairs={{0,12},{4,16},{8,20},{12,24},{16,28},{20,32},{24,36},{28,40},{32,4... | collective-permute-start | bytes 2359304 | tf_op jit(solution)/shard_map/ppermute | solution.py:21
  67.6 39.4 %collective-permute-start.1 = (bf16[2,384,512]{2,1,0:T(8,128)(2,1)}, bf16[2,384,512]{2,1,0:T(8,128)(2,1)}, u32[]{:S(2)}, u32[]{:S(2)}) collective-permute-start(bf16[2,384,512]{2,1,0:T(8,128)(2,1)} %pad_maximum_fusion.3), channel_id=1, source_target_pairs={{0,8},{4,12},{8,16},{12,20},{16,24},{20,28},{24,32},{28,36},{32,40... | collective-permute-start | bytes 2359304 | tf_op jit(solution)/shard_map/ppermute | solution.py:21
  71.9 36.3 %collective-permute-start.2 = (bf16[2,384,512]{2,1,0:T(8,128)(2,1)}, bf16[2,384,512]{2,1,0:T(8,128)(2,1)}, u32[]{:S(2)}, u32[]{:S(2)}) collective-permute-start(bf16[2,384,512]{2,1,0:T(8,128)(2,1)} %pad_maximum_fusion.3), channel_id=1, source_target_pairs={{0,4},{4,8},{8,12},{12,16},{16,20},{20,24},{24,28},{28,32},{32,36}... | collective-permute-start | bytes 2359304 | tf_op jit(solution)/shard_map/ppermute | solution.py:21
  81.9 6.5 %copy-start.8 = (f32[384,1024]{1,0:T(8,128)}, f32[384,1024]{1,0:T(8,128)S(1)}, u32[]{:S(2)}) copy-start(f32[384,1024]{1,0:T(8,128)S(1)} %fusion.36) | copy-start | bytes 4718596
  105.6 79.8 %collective-permute-start.6 = (bf16[384,1920]{0,1:T(8,128)(2,1)}, bf16[384,1920]{0,1:T(8,128)(2,1)S(1)}, u32[]{:S(2)}, u32[]{:S(2)}) collective-permute-start(bf16[384,1920]{0,1:T(8,128)(2,1)} %bitcast.18), channel_id=1, source_target_pairs={{0,4},{4,0},{8,12},{12,8},{16,20},{20,16},{24,28},{28,24},{32,36},... | collective-permute-start | bytes 4423688 | tf_op jit(solution)/shard_map/ppermute | solution.py:229
  136.0 14.6 %collective-permute-start.3 = (bf16[2,384,512]{2,1,0:T(8,128)(2,1)S(1)}, bf16[2,384,512]{2,1,0:T(8,128)(2,1)S(1)}, u32[]{:S(2)}, u32[]{:S(2)}) collective-permute-start(bf16[2,384,512]{2,1,0:T(8,128)(2,1)S(1)} %pad_maximum_fusion.4), channel_id=1, source_target_pairs={{4,0},{8,4},{12,8},{16,12},{20,16},{24,20},{28,24},{32,28},{36,32}... | collective-permute-start | bytes 2359304 | tf_op jit(solution)/shard_map/ppermute | solution.py:21
  137.6 38.5 %collective-permute-start.4 = (bf16[2,384,512]{2,1,0:T(8,128)(2,1)S(1)}, bf16[2,384,512]{2,1,0:T(8,128)(2,1)S(1)}, u32[]{:S(2)}, u32[]{:S(2)}) collective-permute-start(bf16[2,384,512]{2,1,0:T(8,128)(2,1)S(1)} %pad_maximum_fusion.5), channel_id=1, source_target_pairs={{8,0},{12,4},{16,8},{20,12},{24,16},{28,20},{32,24},{36,28},{40,32... | collective-permute-start | bytes 2359304 | tf_op jit(solution)/shard_map/ppermute | solution.py:21
  139.0 38.9 %collective-permute-start.5 = (bf16[2,384,512]{2,1,0:T(8,128)(2,1)S(1)}, bf16[2,384,512]{2,1,0:T(8,128)(2,1)S(1)}, u32[]{:S(2)}, u32[]{:S(2)}) collective-permute-start(bf16[2,384,512]{2,1,0:T(8,128)(2,1)S(1)} %pad_maximum_fusion.6), channel_id=1, source_target_pairs={{12,0},{16,4},{20,8},{24,12},{28,16},{32,20},{36,24},{40,28},{44,3... | collective-permute-start | bytes 2359304 | tf_op jit(solution)/shard_map/ppermute | solution.py:21
  140.3 4.9 %copy-start.28 = (bf16[384,4,4,1,120]{0,4,3,2,1:T(8,128)(2,1)S(1)}, bf16[384,4,4,1,120]{0,4,3,2,1:T(8,128)(2,1)}, u32[]{:S(2)}) copy-start(bf16[384,4,4,1,120]{0,4,3,2,1:T(8,128)(2,1)} %get-tuple-element.26) | copy-start | bytes 4423684
  142.2 43.2 %collective-permute-start.8 = (bf16[384,1024]{1,0:T(8,128)(2,1)}, bf16[384,1024]{1,0:T(8,128)(2,1)}, u32[]{:S(2)}, u32[]{:S(2)}) collective-permute-start(bf16[384,1024]{1,0:T(8,128)(2,1)} %subtract_convert_fusion), channel_id=1, source_target_pairs={{0,4},{4,0},{8,12},{12,8},{16,20},{20,16},{24,28},{28,24},{32,36},... | collective-permute-start | bytes 2359304 | tf_op jit(solution)/shard_map/ppermute | solution.py:318
  189.0 4.8 %copy-start.18 = (f32[384,512]{1,0:T(8,128)S(1)}, f32[384,512]{1,0:T(8,128)}, u32[]{:S(2)}) copy-start(f32[384,512]{1,0:T(8,128)} %copy-done.17) | copy-start | bytes 2359300
  190.3 23.6 %copy-start.4 = (f32[4,4,120,512]{3,2,1,0:T(8,128)}, f32[4,4,120,512]{3,2,1,0:T(8,128)S(1)}, u32[]{:S(2)}) copy-start(f32[4,4,120,512]{3,2,1,0:T(8,128)S(1)} %get-tuple-element.23) | copy-start | bytes 11796484
  190.3 25.5 %copy-start.3 = (f32[4,4,120,512]{3,2,1,0:T(8,128)}, f32[4,4,120,512]{3,2,1,0:T(8,128)S(1)}, u32[]{:S(2)}) copy-start(f32[4,4,120,512]{3,2,1,0:T(8,128)S(1)} %get-tuple-element.24) | copy-start | bytes 11796484
  190.4 23.5 %collective-permute-start.9 = (bf16[4,120,512]{2,1,0:T(8,128)(2,1)S(1)}, bf16[4,120,512]{2,1,0:T(8,128)(2,1)S(1)}, u32[]{:S(2)}, u32[]{:S(2)}) collective-permute-start(bf16[4,120,512]{2,1,0:T(8,128)(2,1)S(1)} %fusion.14), channel_id=1, source_target_pairs={{0,8},{4,12},{8,16},{12,20},{16,24},{20,28},{24,0},{28,4},{32,40},... | collective-permute-start | bytes 1474568 | tf_op jit(solution)/shard_map/ppermute | solution.py:55
  193.7 11.0 %copy-start.29 = (bf16[384,4,4,1,120]{0,4,3,2,1:T(8,128)(2,1)S(1)}, bf16[384,4,4,1,120]{0,4,3,2,1:T(8,128)(2,1)}, u32[]{:S(2)}) copy-start(bf16[384,4,4,1,120]{0,4,3,2,1:T(8,128)(2,1)} %get-tuple-element.26) | copy-start | bytes 4423684
  194.4 26.5 %collective-permute-start.7 = (bf16[384,1024]{1,0:T(8,128)(2,1)S(1)}, bf16[384,1024]{1,0:T(8,128)(2,1)S(1)}, u32[]{:S(2)}, u32[]{:S(2)}) collective-permute-start(bf16[384,1024]{1,0:T(8,128)(2,1)S(1)} %pad_maximum_fusion.8), channel_id=1, source_target_pairs={{0,4},{4,0},{8,12},{12,8},{16,20},{20,16},{24,28},{28,24},{32,36},... | collective-permute-start | bytes 2359304 | tf_op jit(solution)/shard_map/ppermute | solution.py:322
  201.4 14.5 %collective-permute-start.15 = (bf16[4,120,512]{2,1,0:T(8,128)(2,1)S(1)}, bf16[4,120,512]{2,1,0:T(8,128)(2,1)S(1)}, u32[]{:S(2)}, u32[]{:S(2)}) collective-permute-start(bf16[4,120,512]{2,1,0:T(8,128)(2,1)S(1)} %fusion.15), channel_id=1, source_target_pairs={{8,0},{12,4},{16,8},{20,12},{24,16},{28,20},{0,24},{4,28},{40,32},... | collective-permute-start | bytes 1474568 | tf_op jit(solution)/shard_map/ppermute | solution.py:58
  214.8 27.8 %collective-permute-start.10 = (bf16[4,120,512]{2,1,0:T(8,128)(2,1)}, bf16[4,120,512]{2,1,0:T(8,128)(2,1)}, u32[]{:S(2)}, u32[]{:S(2)}) collective-permute-start(bf16[4,120,512]{2,1,0:T(8,128)(2,1)} %fusion.7), channel_id=1, source_target_pairs={{0,8},{4,12},{8,16},{12,20},{16,24},{20,28},{24,0},{28,4},{32,40},... | collective-permute-start | bytes 1474568 | tf_op jit(solution)/shard_map/ppermute | solution.py:55
  216.8 27.4 %collective-permute-start.16 = (bf16[4,120,512]{2,1,0:T(8,128)(2,1)}, bf16[4,120,512]{2,1,0:T(8,128)(2,1)}, u32[]{:S(2)}, u32[]{:S(2)}) collective-permute-start(bf16[4,120,512]{2,1,0:T(8,128)(2,1)} %fusion.5), channel_id=1, source_target_pairs={{8,0},{12,4},{16,8},{20,12},{24,16},{28,20},{0,24},{4,28},{40,32},... | collective-permute-start | bytes 1474568 | tf_op jit(solution)/shard_map/ppermute | solution.py:58
  226.0 8.5 %copy-start.1 = (f32[4,4,120,512]{3,2,1,0:T(8,128)}, f32[4,4,120,512]{3,2,1,0:T(8,128)S(1)}, u32[]{:S(2)}) copy-start(f32[4,4,120,512]{3,2,1,0:T(8,128)S(1)} %get-tuple-element.21) | copy-start | bytes 11796484
  226.1 8.4 %copy-start.15 = (bf16[3840,512]{1,0:T(8,128)(2,1)S(1)}, bf16[3840,512]{1,0:T(8,128)(2,1)}, u32[]{:S(2)}) copy-start(bf16[3840,512]{1,0:T(8,128)(2,1)} %param.10) | copy-start | bytes 11796484
  226.1 22.9 %collective-permute-start.27 = (bf16[4,120,512]{2,1,0:T(8,128)(2,1)S(1)}, bf16[4,120,512]{2,1,0:T(8,128)(2,1)S(1)}, u32[]{:S(2)}, u32[]{:S(2)}) collective-permute-start(bf16[4,120,512]{2,1,0:T(8,128)(2,1)S(1)} %fusion.13), channel_id=1, source_target_pairs={{32,0},{36,4},{40,8},{44,12},{48,16},{52,20},{56,24},{60,28},{64,3... | collective-permute-start | bytes 1474568 | tf_op jit(solution)/shard_map/ppermute | solution.py:58
  241.2 12.9 %copy-start = (f32[4,4,120,512]{3,2,1,0:T(8,128)S(1)}, f32[4,4,120,512]{3,2,1,0:T(8,128)}, u32[]{:S(2)}) copy-start(f32[4,4,120,512]{3,2,1,0:T(8,128)} %get-tuple-element.22) | copy-start | bytes 11796484
  241.2 12.9 %collective-permute-start.21 = (bf16[4,120,512]{2,1,0:T(8,128)(2,1)S(1)}, bf16[4,120,512]{2,1,0:T(8,128)(2,1)S(1)}, u32[]{:S(2)}, u32[]{:S(2)}) collective-permute-start(bf16[4,120,512]{2,1,0:T(8,128)(2,1)S(1)} %fusion.12), channel_id=1, source_target_pairs={{0,32},{4,36},{8,40},{12,44},{16,48},{20,52},{24,56},{28,60},{32,6... | collective-permute-start | bytes 1474568 | tf_op jit(solution)/shard_map/ppermute | solution.py:55
  244.1 13.1 %collective-permute-start.11 = (bf16[4,120,512]{2,1,0:T(8,128)(2,1)S(1)}, bf16[4,120,512]{2,1,0:T(8,128)(2,1)S(1)}, u32[]{:S(2)}, u32[]{:S(2)}) collective-permute-start(bf16[4,120,512]{2,1,0:T(8,128)(2,1)S(1)} %fusion.6), channel_id=1, source_target_pairs={{0,8},{4,12},{8,16},{12,20},{16,24},{20,28},{24,0},{28,4},{32,40},... | collective-permute-start | bytes 1474568 | tf_op jit(solution)/shard_map/ppermute | solution.py:55
  245.7 14.6 %collective-permute-start.17 = (bf16[4,120,512]{2,1,0:T(8,128)(2,1)S(1)}, bf16[4,120,512]{2,1,0:T(8,128)(2,1)S(1)}, u32[]{:S(2)}, u32[]{:S(2)}) collective-permute-start(bf16[4,120,512]{2,1,0:T(8,128)(2,1)S(1)} %fusion.4), channel_id=1, source_target_pairs={{8,0},{12,4},{16,8},{20,12},{24,16},{28,20},{0,24},{4,28},{40,32},... | collective-permute-start | bytes 1474568 | tf_op jit(solution)/shard_map/ppermute | solution.py:58
  250.3 28.7 %collective-permute-start.28 = (bf16[4,120,512]{2,1,0:T(8,128)(2,1)S(1)}, bf16[4,120,512]{2,1,0:T(8,128)(2,1)S(1)}, u32[]{:S(2)}, u32[]{:S(2)}) collective-permute-start(bf16[4,120,512]{2,1,0:T(8,128)(2,1)S(1)} %fusion.9), channel_id=1, source_target_pairs={{32,0},{36,4},{40,8},{44,12},{48,16},{52,20},{56,24},{60,28},{64,3... | collective-permute-start | bytes 1474568 | tf_op jit(solution)/shard_map/ppermute | solution.py:58
  254.3 25.0 %collective-permute-start.22 = (bf16[4,120,512]{2,1,0:T(8,128)(2,1)S(1)}, bf16[4,120,512]{2,1,0:T(8,128)(2,1)S(1)}, u32[]{:S(2)}, u32[]{:S(2)}) collective-permute-start(bf16[4,120,512]{2,1,0:T(8,128)(2,1)S(1)} %fusion.11), channel_id=1, source_target_pairs={{0,32},{4,36},{8,40},{12,44},{16,48},{20,52},{24,56},{28,60},{32,6... | collective-permute-start | bytes 1474568 | tf_op jit(solution)/shard_map/ppermute | solution.py:55
  258.5 20.5 %copy-start.2 = (f32[4,4,120,512]{3,2,1,0:T(8,128)S(1)}, f32[4,4,120,512]{3,2,1,0:T(8,128)}, u32[]{:S(2)}) copy-start(f32[4,4,120,512]{3,2,1,0:T(8,128)} %copy-done.1) | copy-start | bytes 11796484
  258.6 10.6 %collective-permute-start.12 = (bf16[120,512]{1,0:T(8,128)(2,1)S(1)}, bf16[120,512]{1,0:T(8,128)(2,1)S(1)}, u32[]{:S(2)}, u32[]{:S(2)}) collective-permute-start(bf16[120,512]{1,0:T(8,128)(2,1)S(1)} %fusion.29), channel_id=1, source_target_pairs={{0,32},{4,36},{8,40},{12,44},{16,48},{20,52},{24,56},{28,60},{32,6... | collective-permute-start | bytes 368648 | tf_op jit(solution)/shard_map/ppermute | solution.py:55
  261.7 7.5 %collective-permute-start.18 = (bf16[120,512]{1,0:T(8,128)(2,1)S(1)}, bf16[120,512]{1,0:T(8,128)(2,1)S(1)}, u32[]{:S(2)}, u32[]{:S(2)}) collective-permute-start(bf16[120,512]{1,0:T(8,128)(2,1)S(1)} %fusion.30), channel_id=1, source_target_pairs={{32,0},{36,4},{40,8},{44,12},{48,16},{52,20},{56,24},{60,28},{64,3... | collective-permute-start | bytes 368648 | tf_op jit(solution)/shard_map/ppermute | solution.py:58
  269.2 6.2 %collective-permute-start.13 = (bf16[120,512]{1,0:T(8,128)(2,1)S(1)}, bf16[120,512]{1,0:T(8,128)(2,1)S(1)}, u32[]{:S(2)}, u32[]{:S(2)}) collective-permute-start(bf16[120,512]{1,0:T(8,128)(2,1)S(1)} %fusion.28), channel_id=1, source_target_pairs={{0,32},{4,36},{8,40},{12,44},{16,48},{20,52},{24,56},{28,60},{32,6... | collective-permute-start | bytes 368648 | tf_op jit(solution)/shard_map/ppermute | solution.py:55
  269.3 6.1 %collective-permute-start.19 = (bf16[120,512]{1,0:T(8,128)(2,1)S(1)}, bf16[120,512]{1,0:T(8,128)(2,1)S(1)}, u32[]{:S(2)}, u32[]{:S(2)}) collective-permute-start(bf16[120,512]{1,0:T(8,128)(2,1)S(1)} %fusion.25), channel_id=1, source_target_pairs={{32,0},{36,4},{40,8},{44,12},{48,16},{52,20},{56,24},{60,28},{64,3... | collective-permute-start | bytes 368648 | tf_op jit(solution)/shard_map/ppermute | solution.py:58
  275.4 7.5 %collective-permute-start.14 = (bf16[120,512]{1,0:T(8,128)(2,1)S(1)}, bf16[120,512]{1,0:T(8,128)(2,1)S(1)}, u32[]{:S(2)}, u32[]{:S(2)}) collective-permute-start(bf16[120,512]{1,0:T(8,128)(2,1)S(1)} %fusion.27), channel_id=1, source_target_pairs={{0,32},{4,36},{8,40},{12,44},{16,48},{20,52},{24,56},{28,60},{32,6... | collective-permute-start | bytes 368648 | tf_op jit(solution)/shard_map/ppermute | solution.py:55
  275.5 7.4 %collective-permute-start.20 = (bf16[120,512]{1,0:T(8,128)(2,1)S(1)}, bf16[120,512]{1,0:T(8,128)(2,1)S(1)}, u32[]{:S(2)}, u32[]{:S(2)}) collective-permute-start(bf16[120,512]{1,0:T(8,128)(2,1)S(1)} %fusion.24), channel_id=1, source_target_pairs={{32,0},{36,4},{40,8},{44,12},{48,16},{52,20},{56,24},{60,28},{64,3... | collective-permute-start | bytes 368648 | tf_op jit(solution)/shard_map/ppermute | solution.py:58
  279.2 10.1 %collective-permute-start.29 = (bf16[4,120,512]{2,1,0:T(8,128)(2,1)S(1)}, bf16[4,120,512]{2,1,0:T(8,128)(2,1)S(1)}, u32[]{:S(2)}, u32[]{:S(2)}) collective-permute-start(bf16[4,120,512]{2,1,0:T(8,128)(2,1)S(1)} %fusion.8), channel_id=1, source_target_pairs={{32,0},{36,4},{40,8},{44,12},{48,16},{52,20},{56,24},{60,28},{64,3... | collective-permute-start | bytes 1474568 | tf_op jit(solution)/shard_map/ppermute | solution.py:58
  279.5 12.2 %collective-permute-start.23 = (bf16[4,120,512]{2,1,0:T(8,128)(2,1)S(1)}, bf16[4,120,512]{2,1,0:T(8,128)(2,1)S(1)}, u32[]{:S(2)}, u32[]{:S(2)}) collective-permute-start(bf16[4,120,512]{2,1,0:T(8,128)(2,1)S(1)} %fusion.10), channel_id=1, source_target_pairs={{0,32},{4,36},{8,40},{12,44},{16,48},{20,52},{24,56},{28,60},{32,6... | collective-permute-start | bytes 1474568 | tf_op jit(solution)/shard_map/ppermute | solution.py:55
  289.5 6.2 %collective-permute-start.30 = (bf16[120,512]{1,0:T(8,128)(2,1)S(1)}, bf16[120,512]{1,0:T(8,128)(2,1)S(1)}, u32[]{:S(2)}, u32[]{:S(2)}) collective-permute-start(bf16[120,512]{1,0:T(8,128)(2,1)S(1)} %fusion.32), channel_id=1, source_target_pairs={{8,0},{12,4},{16,8},{20,12},{24,16},{28,20},{0,24},{4,28},{40,32},... | collective-permute-start | bytes 368648 | tf_op jit(solution)/shard_map/ppermute | solution.py:58
  291.9 6.8 %collective-permute-start.24 = (bf16[120,512]{1,0:T(8,128)(2,1)S(1)}, bf16[120,512]{1,0:T(8,128)(2,1)S(1)}, u32[]{:S(2)}, u32[]{:S(2)}) collective-permute-start(bf16[120,512]{1,0:T(8,128)(2,1)S(1)} %fusion.31), channel_id=1, source_target_pairs={{0,8},{4,12},{8,16},{12,20},{16,24},{20,28},{24,0},{28,4},{32,40},... | collective-permute-start | bytes 368648 | tf_op jit(solution)/shard_map/ppermute | solution.py:55
  295.7 6.4 %collective-permute-start.31 = (bf16[120,512]{1,0:T(8,128)(2,1)S(1)}, bf16[120,512]{1,0:T(8,128)(2,1)S(1)}, u32[]{:S(2)}, u32[]{:S(2)}) collective-permute-start(bf16[120,512]{1,0:T(8,128)(2,1)S(1)} %fusion.19), channel_id=1, source_target_pairs={{8,0},{12,4},{16,8},{20,12},{24,16},{28,20},{0,24},{4,28},{40,32},... | collective-permute-start | bytes 368648 | tf_op jit(solution)/shard_map/ppermute | solution.py:58
  298.7 7.0 %collective-permute-start.25 = (bf16[120,512]{1,0:T(8,128)(2,1)S(1)}, bf16[120,512]{1,0:T(8,128)(2,1)S(1)}, u32[]{:S(2)}, u32[]{:S(2)}) collective-permute-start(bf16[120,512]{1,0:T(8,128)(2,1)S(1)} %fusion.22), channel_id=1, source_target_pairs={{0,8},{4,12},{8,16},{12,20},{16,24},{20,28},{24,0},{28,4},{32,40},... | collective-permute-start | bytes 368648 | tf_op jit(solution)/shard_map/ppermute | solution.py:55
  302.1 5.9 %collective-permute-start.32 = (bf16[120,512]{1,0:T(8,128)(2,1)S(1)}, bf16[120,512]{1,0:T(8,128)(2,1)S(1)}, u32[]{:S(2)}, u32[]{:S(2)}) collective-permute-start(bf16[120,512]{1,0:T(8,128)(2,1)S(1)} %fusion.18), channel_id=1, source_target_pairs={{8,0},{12,4},{16,8},{20,12},{24,16},{28,20},{0,24},{4,28},{40,32},... | collective-permute-start | bytes 368648 | tf_op jit(solution)/shard_map/ppermute | solution.py:58
  305.8 6.2 %collective-permute-start.26 = (bf16[120,512]{1,0:T(8,128)(2,1)S(1)}, bf16[120,512]{1,0:T(8,128)(2,1)S(1)}, u32[]{:S(2)}, u32[]{:S(2)}) collective-permute-start(bf16[120,512]{1,0:T(8,128)(2,1)S(1)} %fusion.21), channel_id=1, source_target_pairs={{0,8},{4,12},{8,16},{12,20},{16,24},{20,28},{24,0},{28,4},{32,40},... | collective-permute-start | bytes 368648 | tf_op jit(solution)/shard_map/ppermute | solution.py:55
  (24 other events, 73.8 us)
Sparse Core Ops, SparseCore 0:
  9.6 40.2 all-gather.1
  240.1 34.2 reduce-scatter.1
